TPU v7x, 32 devices: a whole 2x2x4 slice. The times are simulated.
32 devices in a mesh: phase: 4 (over y, x), rows: 8 (over z, core).
Axes of the slice: x: 2, y: 2, z: 4, core: 2. Of those that a mesh axis runs over, the one named last changes fastest.
Arguments:
- frames: bfloat16 [2, 192, 16, 128], P(None, None, 'rows'), may hold values from -12 to 12, as said below
- causal_cache: bfloat16 [4, 2, 2, 192, 16, 128], P('phase', None, None, None, 'rows'), may hold values from -4 to 4
- conv_weight: bfloat16 [4, 2, 3, 3, 3, 192, 192], P('phase'), may hold values from -0.15625 to 0.15625
- conv_bias: float32 [4, 2, 192], P('phase'), may hold values from -3 to 3
- norm_gain: float32 [4, 2, 192], P('phase'), may hold values from 0.1 to 1.9
- norm_shift: float32 [4, 2, 192], P('phase'), may hold values from -3 to 3
Outputs:
- phase_out: bfloat16 [4, 2, 192, 16, 128], P('phase', None, None, 'rows')
- new_cache: bfloat16 [4, 2, 2, 192, 16, 128], P('phase', None, None, None, 'rows')
Inputs may be any that keep to these rules, and one draw needn't show every extreme that they name: `frames`: Real-valued frame features.
All inputs are finite; a program needn't handle non-finite values.
Results may differ from a plain program's by a relative error of at most 0.0066.
Values may be sent and summed in bfloat16 or wider, within the bound.
No kernel may reach another device: no remote copies, remote signals or barrier semaphores. Data moves between devices by JAX's collectives and lax.ppermute only.
A program may use at most 64 MiB of HBM per device.

v0:
```python
import jax
import jax.numpy as jnp
from jax import lax
from jax.sharding import PartitionSpec as P

GROUPS = 32


EPS = 1e-06


def with_halo(array, sides, width):
    for axis, dim in sides:
        peers, length = (lax.axis_size(axis), array.shape[dim])
        up = [(i, (i + 1) % peers) for i in range(peers - 1)]
        down = [(j, i) for i, j in up]
        last = lax.slice_in_dim(array, length - width, length, axis=dim)
        leading = lax.slice_in_dim(array, 0, width, axis=dim)
        before = lax.ppermute(last, axis, up)
        after = lax.ppermute(leading, axis, down)
        array = jnp.concatenate([before, array, after], axis=dim)
    return array


def passed_along(value, axis, steps):
    count = lax.axis_size(axis)
    leading, last = (max(0, -steps), min(count, count - steps))
    return lax.ppermute(value, axis, [(source, source + steps) for source in range(leading, last)])


def arrange_taps(weight):
    outputs = weight.shape[3]
    channels = weight.shape[4]
    return jnp.transpose(weight, (2, 3, 0, 1, 4)).reshape(3 * outputs, 9 * channels)


def causal_conv(window, taps, rows_out):
    channels = window.shape[1]
    columns = window.shape[3]
    outputs = taps.shape[0] // 3
    pieces = [
        window[step_t, :, step_y : step_y + rows_out, :]
        for step_t in range(3)
        for step_y in range(3)
    ]
    stacked = jnp.stack(pieces).reshape(9 * channels, rows_out * columns)
    running = jnp.dot(taps, stacked, preferred_element_type=jnp.float32)
    running = running.reshape(3, outputs, rows_out, columns)
    leftward = jnp.pad(running[0, :, :, :-1], ((0, 0), (0, 0), (1, 0)))
    rightward = jnp.pad(running[2, :, :, 1:], ((0, 0), (0, 0), (0, 1)))
    return running[1] + leftward + rightward


def activate(source, gain_vec, shift_vec, keep_rows, cell_count, group_count):
    channels, height, columns = source.shape
    grouped = source.astype(jnp.float32).reshape(
        group_count, channels // group_count, height, columns
    )
    average = lax.psum(jnp.sum(grouped, axis=(1, 2, 3)), "rows") / cell_count
    centred = grouped - average[:, None, None, None]
    spread = lax.psum(jnp.sum(centred * centred, axis=(1, 2, 3)), "rows") / cell_count
    inverse = lax.rsqrt(spread + EPS)
    normed = ((grouped - average[:, None, None, None]) * inverse[:, None, None, None]).reshape(
        channels, height, columns
    )
    normed = normed * gain_vec[:, None, None] + shift_vec[:, None, None]
    return (jax.nn.silu(normed) * keep_rows[None, :, None]).astype(jnp.bfloat16)


def rim_rows(values):
    return with_halo(values, (("rows", 1),), 1)


def run_frame(
    source, first_hist, second_hist, kernels, biases, gains, shifts, group_count, cell_count
):
    rows_here = source.shape[1]
    all_rows = jnp.ones((rows_here,), jnp.float32)
    first_in = rim_rows(activate(source, gains[0], shifts[0], all_rows, cell_count, group_count))
    first_win = jnp.concatenate([first_hist, first_in[None]], axis=0)
    hidden = (causal_conv(first_win, kernels[0], rows_here) + biases[0][:, None, None]).astype(
        jnp.bfloat16
    )
    second_in = rim_rows(activate(hidden, gains[1], shifts[1], all_rows, cell_count, group_count))
    second_win = jnp.concatenate([second_hist, second_in[None]], axis=0)
    result = (
        causal_conv(second_win, kernels[1], rows_here)
        + biases[1][:, None, None]
        + source.astype(jnp.float32)
    )
    return (result.astype(jnp.bfloat16), first_win[1:], second_win[1:])


def shards(frames, causal_cache, conv_weight, conv_bias, norm_gain, norm_shift):
    phase_no = lax.axis_index("phase")
    phase_count = lax.axis_size("phase")
    frame_count = frames.shape[0]
    channels = frames.shape[1]
    rows_here = frames.shape[2]
    columns = frames.shape[3]
    total_rows = rows_here * lax.axis_size("rows")
    cell_count = float(channels // GROUPS * total_rows * columns)
    margin = 1
    cache_flat = causal_cache.reshape(-1, 2, channels, rows_here, columns)
    rimmed = with_halo(cache_flat, (("rows", 3),), margin)
    local_taps = (arrange_taps(conv_weight[0, 0]), arrange_taps(conv_weight[0, 1]))
    first_hist = rimmed[0]
    second_hist = rimmed[1, :, :, margin - 1 : margin + 1 + rows_here, :]
    incoming = jnp.zeros_like(frames[0])
    produced = jnp.zeros_like(frames)
    tick_count = frame_count + phase_count - 1
    for tick_no in range(tick_count):
        frame_no = tick_no - phase_no
        active_now = jnp.logical_and(frame_no >= 0, frame_no < frame_count)
        source = jnp.where(phase_no == 0, frames[min(tick_no, frame_count - 1)], incoming)
        result, first_next, second_next = run_frame(
            source,
            first_hist,
            second_hist,
            local_taps,
            conv_bias[0],
            norm_gain[0],
            norm_shift[0],
            GROUPS,
            cell_count,
        )
        first_hist = jnp.where(active_now, first_next, first_hist)
        second_hist = jnp.where(active_now, second_next, second_hist)
        frame_slot = jnp.clip(frame_no, 0, frame_count - 1)
        produced = jnp.where(
            active_now, lax.dynamic_update_index_in_dim(produced, result, frame_slot, 0), produced
        )
        if tick_no + 1 < tick_count:
            incoming = passed_along(result, "phase", 1)
    new_cache = jnp.stack(
        [first_hist[:, :, margin : margin + rows_here, :], second_hist[:, :, 1 : 1 + rows_here, :]]
    )
    return (produced[None], new_cache[None])


def solution(mesh):
    in_specs = (
        P(None, None, "rows", None),
        P("phase", None, None, None, "rows", None),
        P("phase", None, None, None, None, None, None),
        P("phase", None, None),
        P("phase", None, None),
        P("phase", None, None),
    )
    out_specs = (P("phase", None, None, "rows", None), P("phase", None, None, None, "rows", None))
    return jax.shard_map(shards, mesh=mesh, in_specs=in_specs, out_specs=out_specs, check_vma=False)
```

profile of v0, /device:TPU:12, one launch (start us, length us, event | category | flops | bytes accessed | tf_op | source)
XLA Modules:
  0.0 478.8 jit_solution(14762591676880482576)
XLA Ops:
  11.1 13.2 %psum.140 = f32[32]{0:T(128)S(1)} all-reduce(f32[32]{0:T(128)S(1)} %reduce_sum.235), channel_id=1, replica_groups=mesh['phase'=4,'rows'=8] {'rows'}, use_global_device_ids=true, to_apply=%region_2.3 | all-reduce | flops 32 | bytes 256 | tf_op jit(solution)/shard_map/psum | solution.py:59
  25.0 13.6 %psum.141 = f32[32]{0:T(128)S(1)} all-reduce(f32[32]{0:T(128)S(1)} %reduce_sum.241), channel_id=1, replica_groups=mesh['phase'=4,'rows'=8] {'rows'}, use_global_device_ids=true, to_apply=%region_5.6 | all-reduce | flops 32 | bytes 256 | tf_op jit(solution)/shard_map/psum | solution.py:61
  40.2 5.5 %collective-permute-start.3 = (bf16[192,1,128]{2,0,1:T(8,128)(2,1)}, bf16[192,1,128]{2,0,1:T(8,128)(2,1)}, u32[]{:S(2)}, u32[]{:S(2)}) collective-permute-start(bf16[192,1,128]{2,0,1:T(8,128)(2,1)} %get-tuple-element.79), channel_id=1, source_target_pairs={{1,0},{2,1},{3,2},{4,3},{5,4},{6,5},{7,6},{9,8},{10,9},{11,10},{12... | collective-permute-start | bytes 147464 | tf_op jit(solution)/shard_map/ppermute | solution.py:20
  47.6 5.5 %slice_bitcast_fusion.1 = (bf16[3,192,3,3,192]{4,1,0,3,2:T(8,128)(2,1)}, bf16[3,192,3,3,192]{4,1,0,3,2:T(8,128)(2,1)}) fusion(bf16[1,2,3,3,3,192,192]{6,5,4,3,2,1,0:T(8,128)(2,1)} %param.8), kind=kLoop, calls=%fused_computation.1 | loop fusion | bytes 7962624 | tf_op jit(solution)/shard_map/transpose | solution.py:34
  53.7 4.0 copy.25
  57.7 4.2 reshape.216
  62.0 4.0 copy.20
  66.0 4.2 reshape.213
  76.0 11.7 %psum.142 = f32[32]{0:T(128)S(1)} all-reduce(f32[32]{0:T(128)S(1)} %reduce_sum.247), channel_id=1, replica_groups=mesh['phase'=4,'rows'=8] {'rows'}, use_global_device_ids=true, to_apply=%region_8.9 | all-reduce | flops 32 | bytes 256 | tf_op jit(solution)/shard_map/psum | solution.py:59
  88.3 13.6 %psum.143 = f32[32]{0:T(128)S(1)} all-reduce(f32[32]{0:T(128)S(1)} %reduce_sum.250), channel_id=1, replica_groups=mesh['phase'=4,'rows'=8] {'rows'}, use_global_device_ids=true, to_apply=%region_11.12 | all-reduce | flops 32 | bytes 256 | tf_op jit(solution)/shard_map/psum | solution.py:61
  102.3 5.4 %collective-permute-start.5 = (bf16[192,1,128]{2,0,1:T(8,128)(2,1)S(1)}, bf16[192,1,128]{2,0,1:T(8,128)(2,1)S(1)}, u32[]{:S(2)}, u32[]{:S(2)}) collective-permute-start(bf16[192,1,128]{2,0,1:T(8,128)(2,1)S(1)} %get-tuple-element.77), channel_id=1, source_target_pairs={{1,0},{2,1},{3,2},{4,3},{5,4},{6,5},{7,6},{9,8},{10,9},{11,10},{12... | collective-permute-start | bytes 147464 | tf_op jit(solution)/shard_map/ppermute | solution.py:20
  110.0 3.1 collective-permute-done.4
  117.7 3.4 collective-permute-start.6
  121.3 3.9 collective-permute-done.6
  125.5 10.0 %psum.144 = f32[32]{0:T(128)S(1)} all-reduce(f32[32]{0:T(128)S(1)} %reduce_sum.256), channel_id=1, replica_groups=mesh['phase'=4,'rows'=8] {'rows'}, use_global_device_ids=true, to_apply=%region_14.15 | all-reduce | flops 32 | bytes 256 | tf_op jit(solution)/shard_map/psum | solution.py:59
  136.1 13.0 %psum.145 = f32[32]{0:T(128)S(1)} all-reduce(f32[32]{0:T(128)S(1)} %reduce_sum.262), channel_id=1, replica_groups=mesh['phase'=4,'rows'=8] {'rows'}, use_global_device_ids=true, to_apply=%region_17.18 | all-reduce | flops 32 | bytes 256 | tf_op jit(solution)/shard_map/psum | solution.py:61
  149.6 5.5 %collective-permute-start.8 = (bf16[192,1,128]{2,0,1:T(8,128)(2,1)S(1)}, bf16[192,1,128]{2,0,1:T(8,128)(2,1)S(1)}, u32[]{:S(2)}, u32[]{:S(2)}) collective-permute-start(bf16[192,1,128]{2,0,1:T(8,128)(2,1)S(1)} %get-tuple-element.75), channel_id=1, source_target_pairs={{1,0},{2,1},{3,2},{4,3},{5,4},{6,5},{7,6},{9,8},{10,9},{11,10},{12... | collective-permute-start | bytes 147464 | tf_op jit(solution)/shard_map/ppermute | solution.py:20
  157.6 2.8 collective-permute-done.7
  164.9 10.0 %psum.146 = f32[32]{0:T(128)S(1)} all-reduce(f32[32]{0:T(128)S(1)} %reduce_sum.265), channel_id=1, replica_groups=mesh['phase'=4,'rows'=8] {'rows'}, use_global_device_ids=true, to_apply=%region_20.21 | all-reduce | flops 32 | bytes 256 | tf_op jit(solution)/shard_map/psum | solution.py:59
  175.5 12.9 %psum.147 = f32[32]{0:T(128)S(1)} all-reduce(f32[32]{0:T(128)S(1)} %reduce_sum.271), channel_id=1, replica_groups=mesh['phase'=4,'rows'=8] {'rows'}, use_global_device_ids=true, to_apply=%region_23.24 | all-reduce | flops 32 | bytes 256 | tf_op jit(solution)/shard_map/psum | solution.py:61
  188.8 5.5 %collective-permute-start.10 = (bf16[192,1,128]{2,0,1:T(8,128)(2,1)S(1)}, bf16[192,1,128]{2,0,1:T(8,128)(2,1)S(1)}, u32[]{:S(2)}, u32[]{:S(2)}) collective-permute-start(bf16[192,1,128]{2,0,1:T(8,128)(2,1)S(1)} %get-tuple-element.73), channel_id=1, source_target_pairs={{1,0},{2,1},{3,2},{4,3},{5,4},{6,5},{7,6},{9,8},{10,9},{11,10},{12... | collective-permute-start | bytes 147464 | tf_op jit(solution)/shard_map/ppermute | solution.py:20
  196.5 3.3 collective-permute-done.9
  207.1 3.9 collective-permute-done.11
  211.3 10.3 %psum.148 = f32[32]{0:T(128)S(1)} all-reduce(f32[32]{0:T(128)S(1)} %reduce_sum.277), channel_id=1, replica_groups=mesh['phase'=4,'rows'=8] {'rows'}, use_global_device_ids=true, to_apply=%region_26.27 | all-reduce | flops 32 | bytes 256 | tf_op jit(solution)/shard_map/psum | solution.py:59
  222.2 12.4 %psum.149 = f32[32]{0:T(128)S(1)} all-reduce(f32[32]{0:T(128)S(1)} %reduce_sum.280), channel_id=1, replica_groups=mesh['phase'=4,'rows'=8] {'rows'}, use_global_device_ids=true, to_apply=%region_29.30 | all-reduce | flops 32 | bytes 256 | tf_op jit(solution)/shard_map/psum | solution.py:61
  235.1 5.5 %collective-permute-start.13 = (bf16[192,1,128]{2,0,1:T(8,128)(2,1)S(1)}, bf16[192,1,128]{2,0,1:T(8,128)(2,1)S(1)}, u32[]{:S(2)}, u32[]{:S(2)}) collective-permute-start(bf16[192,1,128]{2,0,1:T(8,128)(2,1)S(1)} %get-tuple-element.71), channel_id=1, source_target_pairs={{1,0},{2,1},{3,2},{4,3},{5,4},{6,5},{7,6},{9,8},{10,9},{11,10},{12... | collective-permute-start | bytes 147464 | tf_op jit(solution)/shard_map/ppermute | solution.py:20
  243.3 2.6 collective-permute-done.12
  250.4 10.0 %psum.150 = f32[32]{0:T(128)S(1)} all-reduce(f32[32]{0:T(128)S(1)} %reduce_sum.286), channel_id=1, replica_groups=mesh['phase'=4,'rows'=8] {'rows'}, use_global_device_ids=true, to_apply=%region_32.33 | all-reduce | flops 32 | bytes 256 | tf_op jit(solution)/shard_map/psum | solution.py:59
  261.0 12.9 %psum.151 = f32[32]{0:T(128)S(1)} all-reduce(f32[32]{0:T(128)S(1)} %reduce_sum.292), channel_id=1, replica_groups=mesh['phase'=4,'rows'=8] {'rows'}, use_global_device_ids=true, to_apply=%region_35.36 | all-reduce | flops 32 | bytes 256 | tf_op jit(solution)/shard_map/psum | solution.py:61
  274.3 5.5 %collective-permute-start.15 = (bf16[192,1,128]{2,0,1:T(8,128)(2,1)S(1)}, bf16[192,1,128]{2,0,1:T(8,128)(2,1)S(1)}, u32[]{:S(2)}, u32[]{:S(2)}) collective-permute-start(bf16[192,1,128]{2,0,1:T(8,128)(2,1)S(1)} %get-tuple-element.69), channel_id=1, source_target_pairs={{1,0},{2,1},{3,2},{4,3},{5,4},{6,5},{7,6},{9,8},{10,9},{11,10},{12... | collective-permute-start | bytes 147464 | tf_op jit(solution)/shard_map/ppermute | solution.py:20
  282.0 3.3 collective-permute-done.14
  291.1 5.4 %collective-permute-done.16 = bf16[192,2,128]{2,0,1:T(8,128)(2,1)S(1)} collective-permute-done((bf16[192,2,128]{2,0,1:T(8,128)(2,1)S(1)}, bf16[192,2,128]{2,0,1:T(8,128)(2,1)S(1)}, u32[]{:S(2)}, u32[]{:S(2)}) %collective-permute-start.16) | collective-permute-done | bytes 98336 | tf_op jit(solution)/shard_map/ppermute | solution.py:28
  296.8 10.3 %psum.152 = f32[32]{0:T(128)S(1)} all-reduce(f32[32]{0:T(128)S(1)} %reduce_sum.295), channel_id=1, replica_groups=mesh['phase'=4,'rows'=8] {'rows'}, use_global_device_ids=true, to_apply=%region_38.39 | all-reduce | flops 32 | bytes 256 | tf_op jit(solution)/shard_map/psum | solution.py:59
  307.8 12.4 %psum.153 = f32[32]{0:T(128)S(1)} all-reduce(f32[32]{0:T(128)S(1)} %reduce_sum.361), channel_id=1, replica_groups=mesh['phase'=4,'rows'=8] {'rows'}, use_global_device_ids=true, to_apply=%region_41.42 | all-reduce | flops 32 | bytes 256 | tf_op jit(solution)/shard_map/psum | solution.py:61
  320.6 5.5 %collective-permute-start.18 = (bf16[192,1,128]{2,0,1:T(8,128)(2,1)S(1)}, bf16[192,1,128]{2,0,1:T(8,128)(2,1)S(1)}, u32[]{:S(2)}, u32[]{:S(2)}) collective-permute-start(bf16[192,1,128]{2,0,1:T(8,128)(2,1)S(1)} %get-tuple-element.67), channel_id=1, source_target_pairs={{1,0},{2,1},{3,2},{4,3},{5,4},{6,5},{7,6},{9,8},{10,9},{11,10},{12... | collective-permute-start | bytes 147464 | tf_op jit(solution)/shard_map/ppermute | solution.py:20
  329.0 2.5 collective-permute-done.17
  335.9 10.0 %psum.154 = f32[32]{0:T(128)S(1)} all-reduce(f32[32]{0:T(128)S(1)} %reduce_sum.364), channel_id=1, replica_groups=mesh['phase'=4,'rows'=8] {'rows'}, use_global_device_ids=true, to_apply=%region_44.45 | all-reduce | flops 32 | bytes 256 | tf_op jit(solution)/shard_map/psum | solution.py:59
  346.5 12.9 %psum.155 = f32[32]{0:T(128)S(1)} all-reduce(f32[32]{0:T(128)S(1)} %reduce_sum.367), channel_id=1, replica_groups=mesh['phase'=4,'rows'=8] {'rows'}, use_global_device_ids=true, to_apply=%region_47.48 | all-reduce | flops 32 | bytes 256 | tf_op jit(solution)/shard_map/psum | solution.py:61
  359.9 5.5 %collective-permute-start.20 = (bf16[192,1,128]{2,0,1:T(8,128)(2,1)S(1)}, bf16[192,1,128]{2,0,1:T(8,128)(2,1)S(1)}, u32[]{:S(2)}, u32[]{:S(2)}) collective-permute-start(bf16[192,1,128]{2,0,1:T(8,128)(2,1)S(1)} %get-tuple-element.65), channel_id=1, source_target_pairs={{1,0},{2,1},{3,2},{4,3},{5,4},{6,5},{7,6},{9,8},{10,9},{11,10},{12... | collective-permute-start | bytes 147464 | tf_op jit(solution)/shard_map/ppermute | solution.py:20
  367.7 3.0 collective-permute-done.19
  383.1 5.4 %collective-permute-done.21 = bf16[192,2,128]{2,0,1:T(8,128)(2,1)S(1)} collective-permute-done((bf16[192,2,128]{2,0,1:T(8,128)(2,1)S(1)}, bf16[192,2,128]{2,0,1:T(8,128)(2,1)S(1)}, u32[]{:S(2)}, u32[]{:S(2)}) %collective-permute-start.21) | collective-permute-done | bytes 98336 | tf_op jit(solution)/shard_map/ppermute | solution.py:28
  388.8 10.0 %psum.156 = f32[32]{0:T(128)S(1)} all-reduce(f32[32]{0:T(128)S(1)} %reduce_sum.370), channel_id=1, replica_groups=mesh['phase'=4,'rows'=8] {'rows'}, use_global_device_ids=true, to_apply=%region_50.51 | all-reduce | flops 32 | bytes 256 | tf_op jit(solution)/shard_map/psum | solution.py:59
  399.5 13.0 %psum.157 = f32[32]{0:T(128)S(1)} all-reduce(f32[32]{0:T(128)S(1)} %reduce_sum.373), channel_id=1, replica_groups=mesh['phase'=4,'rows'=8] {'rows'}, use_global_device_ids=true, to_apply=%region_53.54 | all-reduce | flops 32 | bytes 256 | tf_op jit(solution)/shard_map/psum | solution.py:61
  413.7 5.5 %collective-permute-start.23 = (bf16[192,1,128]{2,0,1:T(8,128)(2,1)S(1)}, bf16[192,1,128]{2,0,1:T(8,128)(2,1)S(1)}, u32[]{:S(2)}, u32[]{:S(2)}) collective-permute-start(bf16[192,1,128]{2,0,1:T(8,128)(2,1)S(1)} %get-tuple-element.63), channel_id=1, source_target_pairs={{1,0},{2,1},{3,2},{4,3},{5,4},{6,5},{7,6},{9,8},{10,9},{11,10},{12... | collective-permute-start | bytes 147464 | tf_op jit(solution)/shard_map/ppermute | solution.py:20
  435.0 10.3 %psum.158 = f32[32]{0:T(128)S(1)} all-reduce(f32[32]{0:T(128)S(1)} %reduce_sum.376), channel_id=1, replica_groups=mesh['phase'=4,'rows'=8] {'rows'}, use_global_device_ids=true, to_apply=%region_56.57 | all-reduce | flops 32 | bytes 256 | tf_op jit(solution)/shard_map/psum | solution.py:59
  445.9 12.8 %psum.159 = f32[32]{0:T(128)S(1)} all-reduce(f32[32]{0:T(128)S(1)} %reduce_sum.379), channel_id=1, replica_groups=mesh['phase'=4,'rows'=8] {'rows'}, use_global_device_ids=true, to_apply=%region_59.60 | all-reduce | flops 32 | bytes 256 | tf_op jit(solution)/shard_map/psum | solution.py:61
  459.1 5.6 %collective-permute-start.25 = (bf16[192,1,128]{2,0,1:T(8,128)(2,1)S(1)}, bf16[192,1,128]{2,0,1:T(8,128)(2,1)S(1)}, u32[]{:S(2)}, u32[]{:S(2)}) collective-permute-start(bf16[192,1,128]{2,0,1:T(8,128)(2,1)S(1)} %get-tuple-element.61), channel_id=1, source_target_pairs={{1,0},{2,1},{3,2},{4,3},{5,4},{6,5},{7,6},{9,8},{10,9},{11,10},{12... | collective-permute-start | bytes 147464 | tf_op jit(solution)/shard_map/ppermute | solution.py:20
  467.4 2.8 collective-permute-done.24
  (434 shorter events, 118.1 us)
Async XLA Ops:
  3.2 68.0 %collective-permute-start.1 = (bf16[2,2,192,1,128]{4,2,3,1,0:T(8,128)(2,1)}, bf16[2,2,192,1,128]{4,2,3,1,0:T(8,128)(2,1)}, u32[]{:S(2)}, u32[]{:S(2)}) collective-permute-start(bf16[2,2,192,1,128]{4,2,3,1,0:T(8,128)(2,1)} %get-tuple-element.57), channel_id=1, source_target_pairs={{1,0},{2,1},{3,2},{4,3},{5,4},{6,5},{7,6},{9,8},{10,9},{11,10},{12... | collective-permute-start | bytes 589832 | tf_op jit(solution)/shard_map/ppermute | solution.py:20
  5.1 66.1 %collective-permute-start = (bf16[2,2,192,1,128]{4,2,3,1,0:T(8,128)(2,1)}, bf16[2,2,192,1,128]{4,2,3,1,0:T(8,128)(2,1)}, u32[]{:S(2)}, u32[]{:S(2)}) collective-permute-start(bf16[2,2,192,1,128]{4,2,3,1,0:T(8,128)(2,1)} %get-tuple-element.56), channel_id=1, source_target_pairs={{0,1},{1,2},{2,3},{3,4},{4,5},{5,6},{6,7},{8,9},{9,10},{10,11},{11... | collective-permute-start | bytes 589832 | tf_op jit(solution)/shard_map/ppermute | solution.py:19
  9.2 43.9 %copy-start.1 = (bf16[1,192,2,128]{3,2,1,0:T(2,128)(2,1)}, bf16[1,192,2,128]{3,2,1,0:T(2,128)(2,1)S(1)}, u32[]{:S(2)}) copy-start(bf16[1,192,2,128]{3,2,1,0:T(2,128)(2,1)S(1)} %get-tuple-element.59) | copy-start | bytes 294916
  10.8 36.9 %copy-start.33 = (f32[1,1,192]{2,1,0:T(1,128)}, f32[1,1,192]{2,1,0:T(1,128)S(1)}, u32[]{:S(2)}) copy-start(f32[1,1,192]{2,1,0:T(1,128)S(1)} %get-tuple-element.81) | copy-start | bytes 2308
  40.2 30.0 %collective-permute-start.3 = (bf16[192,1,128]{2,0,1:T(8,128)(2,1)}, bf16[192,1,128]{2,0,1:T(8,128)(2,1)}, u32[]{:S(2)}, u32[]{:S(2)}) collective-permute-start(bf16[192,1,128]{2,0,1:T(8,128)(2,1)} %get-tuple-element.79), channel_id=1, source_target_pairs={{1,0},{2,1},{3,2},{4,3},{5,4},{6,5},{7,6},{9,8},{10,9},{11,10},{12... | collective-permute-start | bytes 147464 | tf_op jit(solution)/shard_map/ppermute | solution.py:20
  45.7 7.4 %copy-start.38 = (f32[1,2,192]{2,1,0:T(2,128)S(1)}, f32[1,2,192]{2,1,0:T(2,128)}, u32[]{:S(2)}) copy-start(f32[1,2,192]{2,1,0:T(2,128)} %param.9) | copy-start | bytes 4612
  45.7 24.5 %collective-permute-start.2 = (bf16[192,1,128]{2,0,1:T(8,128)(2,1)}, bf16[192,1,128]{2,0,1:T(8,128)(2,1)}, u32[]{:S(2)}, u32[]{:S(2)}) collective-permute-start(bf16[192,1,128]{2,0,1:T(8,128)(2,1)} %get-tuple-element.78), channel_id=1, source_target_pairs={{0,1},{1,2},{2,3},{3,4},{4,5},{5,6},{6,7},{8,9},{9,10},{10,11},{11... | collective-permute-start | bytes 147464 | tf_op jit(solution)/shard_map/ppermute | solution.py:19
  102.3 7.7 %collective-permute-start.5 = (bf16[192,1,128]{2,0,1:T(8,128)(2,1)S(1)}, bf16[192,1,128]{2,0,1:T(8,128)(2,1)S(1)}, u32[]{:S(2)}, u32[]{:S(2)}) collective-permute-start(bf16[192,1,128]{2,0,1:T(8,128)(2,1)S(1)} %get-tuple-element.77), channel_id=1, source_target_pairs={{1,0},{2,1},{3,2},{4,3},{5,4},{6,5},{7,6},{9,8},{10,9},{11,10},{12... | collective-permute-start | bytes 147464 | tf_op jit(solution)/shard_map/ppermute | solution.py:20
  107.7 5.4 %collective-permute-start.4 = (bf16[192,1,128]{2,0,1:T(8,128)(2,1)S(1)}, bf16[192,1,128]{2,0,1:T(8,128)(2,1)S(1)}, u32[]{:S(2)}, u32[]{:S(2)}) collective-permute-start(bf16[192,1,128]{2,0,1:T(8,128)(2,1)S(1)} %get-tuple-element.76), channel_id=1, source_target_pairs={{0,1},{1,2},{2,3},{3,4},{4,5},{5,6},{6,7},{8,9},{9,10},{10,11},{11... | collective-permute-start | bytes 147464 | tf_op jit(solution)/shard_map/ppermute | solution.py:19
  109.9 4.2 copy-start.4
  116.0 9.1 %copy-start.3 = (bf16[1,192,2,128]{3,2,1,0:T(2,128)(2,1)S(1)}, bf16[1,192,2,128]{3,2,1,0:T(2,128)(2,1)}, u32[]{:S(2)}) copy-start(bf16[1,192,2,128]{3,2,1,0:T(2,128)(2,1)} %get-tuple-element.58) | copy-start | bytes 294916
  116.0 33.3 %copy-start.34 = (f32[1,1,192]{2,1,0:T(1,128)S(1)}, f32[1,1,192]{2,1,0:T(1,128)}, u32[]{:S(2)}) copy-start(f32[1,1,192]{2,1,0:T(1,128)} %copy-done.33) | copy-start | bytes 2308
  116.3 44.1 %copy-start.13 = (bf16[9,192,2,128]{3,1,2,0:T(8,128)(2,1)S(1)}, bf16[9,192,2,128]{3,1,2,0:T(8,128)(2,1)}, u32[]{:S(2)}) copy-start(bf16[9,192,2,128]{3,1,2,0:T(8,128)(2,1)} %copy-done.12) | copy-start | bytes 2654212
  117.7 7.4 %collective-permute-start.6 = (bf16[192,2,128]{2,0,1:T(8,128)(2,1)S(1)}, bf16[192,2,128]{2,0,1:T(8,128)(2,1)S(1)}, u32[]{:S(2)}, u32[]{:S(2)}) collective-permute-start(bf16[192,2,128]{2,0,1:T(8,128)(2,1)S(1)} %get-tuple-element.29), channel_id=1, source_target_pairs={{0,8},{8,16},{16,24},{1,9},{9,17},{17,25},{2,10},{10,18},{18,26},{... | collective-permute-start | bytes 294920 | tf_op jit(solution)/shard_map/ppermute | solution.py:28
  121.2 3.9 copy-start.14
  149.6 8.0 %collective-permute-start.8 = (bf16[192,1,128]{2,0,1:T(8,128)(2,1)S(1)}, bf16[192,1,128]{2,0,1:T(8,128)(2,1)S(1)}, u32[]{:S(2)}, u32[]{:S(2)}) collective-permute-start(bf16[192,1,128]{2,0,1:T(8,128)(2,1)S(1)} %get-tuple-element.75), channel_id=1, source_target_pairs={{1,0},{2,1},{3,2},{4,3},{5,4},{6,5},{7,6},{9,8},{10,9},{11,10},{12... | collective-permute-start | bytes 147464 | tf_op jit(solution)/shard_map/ppermute | solution.py:20
  155.0 5.4 %collective-permute-start.7 = (bf16[192,1,128]{2,0,1:T(8,128)(2,1)S(1)}, bf16[192,1,128]{2,0,1:T(8,128)(2,1)S(1)}, u32[]{:S(2)}, u32[]{:S(2)}) collective-permute-start(bf16[192,1,128]{2,0,1:T(8,128)(2,1)S(1)} %get-tuple-element.74), channel_id=1, source_target_pairs={{0,1},{1,2},{2,3},{3,4},{4,5},{5,6},{6,7},{8,9},{9,10},{10,11},{11... | collective-permute-start | bytes 147464 | tf_op jit(solution)/shard_map/ppermute | solution.py:19
  175.0 24.8 %copy-start.15 = (bf16[9,192,2,128]{3,1,2,0:T(8,128)(2,1)S(1)}, bf16[9,192,2,128]{3,1,2,0:T(8,128)(2,1)}, u32[]{:S(2)}) copy-start(bf16[9,192,2,128]{3,1,2,0:T(8,128)(2,1)} %constant_dynamic-update-slice_fusion.30) | copy-start | bytes 2654212
  188.8 7.6 %collective-permute-start.10 = (bf16[192,1,128]{2,0,1:T(8,128)(2,1)S(1)}, bf16[192,1,128]{2,0,1:T(8,128)(2,1)S(1)}, u32[]{:S(2)}, u32[]{:S(2)}) collective-permute-start(bf16[192,1,128]{2,0,1:T(8,128)(2,1)S(1)} %get-tuple-element.73), channel_id=1, source_target_pairs={{1,0},{2,1},{3,2},{4,3},{5,4},{6,5},{7,6},{9,8},{10,9},{11,10},{12... | collective-permute-start | bytes 147464 | tf_op jit(solution)/shard_map/ppermute | solution.py:20
  194.3 5.4 %collective-permute-start.9 = (bf16[192,1,128]{2,0,1:T(8,128)(2,1)S(1)}, bf16[192,1,128]{2,0,1:T(8,128)(2,1)S(1)}, u32[]{:S(2)}, u32[]{:S(2)}) collective-permute-start(bf16[192,1,128]{2,0,1:T(8,128)(2,1)S(1)} %get-tuple-element.72), channel_id=1, source_target_pairs={{0,1},{1,2},{2,3},{3,4},{4,5},{5,6},{6,7},{8,9},{9,10},{10,11},{11... | collective-permute-start | bytes 147464 | tf_op jit(solution)/shard_map/ppermute | solution.py:19
  196.4 4.4 copy-start.5
  202.3 43.7 %copy-start.17 = (bf16[9,192,2,128]{3,1,2,0:T(8,128)(2,1)S(1)}, bf16[9,192,2,128]{3,1,2,0:T(8,128)(2,1)}, u32[]{:S(2)}) copy-start(bf16[9,192,2,128]{3,1,2,0:T(8,128)(2,1)} %copy-done.16) | copy-start | bytes 2654212
  203.6 7.4 %collective-permute-start.11 = (bf16[192,2,128]{2,0,1:T(8,128)(2,1)S(1)}, bf16[192,2,128]{2,0,1:T(8,128)(2,1)S(1)}, u32[]{:S(2)}, u32[]{:S(2)}) collective-permute-start(bf16[192,2,128]{2,0,1:T(8,128)(2,1)S(1)} %get-tuple-element.23), channel_id=1, source_target_pairs={{0,8},{8,16},{16,24},{1,9},{9,17},{17,25},{2,10},{10,18},{18,26},{... | collective-permute-start | bytes 294920 | tf_op jit(solution)/shard_map/ppermute | solution.py:28
  235.1 8.3 %collective-permute-start.13 = (bf16[192,1,128]{2,0,1:T(8,128)(2,1)S(1)}, bf16[192,1,128]{2,0,1:T(8,128)(2,1)S(1)}, u32[]{:S(2)}, u32[]{:S(2)}) collective-permute-start(bf16[192,1,128]{2,0,1:T(8,128)(2,1)S(1)} %get-tuple-element.71), channel_id=1, source_target_pairs={{1,0},{2,1},{3,2},{4,3},{5,4},{6,5},{7,6},{9,8},{10,9},{11,10},{12... | collective-permute-start | bytes 147464 | tf_op jit(solution)/shard_map/ppermute | solution.py:20
  240.6 5.4 %collective-permute-start.12 = (bf16[192,1,128]{2,0,1:T(8,128)(2,1)S(1)}, bf16[192,1,128]{2,0,1:T(8,128)(2,1)S(1)}, u32[]{:S(2)}, u32[]{:S(2)}) collective-permute-start(bf16[192,1,128]{2,0,1:T(8,128)(2,1)S(1)} %get-tuple-element.70), channel_id=1, source_target_pairs={{0,1},{1,2},{2,3},{3,4},{4,5},{5,6},{6,7},{8,9},{9,10},{10,11},{11... | collective-permute-start | bytes 147464 | tf_op jit(solution)/shard_map/ppermute | solution.py:19
  260.5 24.8 %copy-start.19 = (bf16[9,192,2,128]{3,1,2,0:T(8,128)(2,1)S(1)}, bf16[9,192,2,128]{3,1,2,0:T(8,128)(2,1)}, u32[]{:S(2)}) copy-start(bf16[9,192,2,128]{3,1,2,0:T(8,128)(2,1)} %constant_dynamic-update-slice_fusion.48) | copy-start | bytes 2654212
  274.3 7.6 %collective-permute-start.15 = (bf16[192,1,128]{2,0,1:T(8,128)(2,1)S(1)}, bf16[192,1,128]{2,0,1:T(8,128)(2,1)S(1)}, u32[]{:S(2)}, u32[]{:S(2)}) collective-permute-start(bf16[192,1,128]{2,0,1:T(8,128)(2,1)S(1)} %get-tuple-element.69), channel_id=1, source_target_pairs={{1,0},{2,1},{3,2},{4,3},{5,4},{6,5},{7,6},{9,8},{10,9},{11,10},{12... | collective-permute-start | bytes 147464 | tf_op jit(solution)/shard_map/ppermute | solution.py:20
  279.8 5.4 %collective-permute-start.14 = (bf16[192,1,128]{2,0,1:T(8,128)(2,1)S(1)}, bf16[192,1,128]{2,0,1:T(8,128)(2,1)S(1)}, u32[]{:S(2)}, u32[]{:S(2)}) collective-permute-start(bf16[192,1,128]{2,0,1:T(8,128)(2,1)S(1)} %get-tuple-element.68), channel_id=1, source_target_pairs={{0,1},{1,2},{2,3},{3,4},{4,5},{5,6},{6,7},{8,9},{9,10},{10,11},{11... | collective-permute-start | bytes 147464 | tf_op jit(solution)/shard_map/ppermute | solution.py:19
  281.9 4.4 copy-start.6
  287.8 43.7 %copy-start.21 = (bf16[9,192,2,128]{3,1,2,0:T(8,128)(2,1)S(1)}, bf16[9,192,2,128]{3,1,2,0:T(8,128)(2,1)}, u32[]{:S(2)}) copy-start(bf16[9,192,2,128]{3,1,2,0:T(8,128)(2,1)} %copy-done.20) | copy-start | bytes 2654212
  289.1 7.4 %collective-permute-start.16 = (bf16[192,2,128]{2,0,1:T(8,128)(2,1)S(1)}, bf16[192,2,128]{2,0,1:T(8,128)(2,1)S(1)}, u32[]{:S(2)}, u32[]{:S(2)}) collective-permute-start(bf16[192,2,128]{2,0,1:T(8,128)(2,1)S(1)} %get-tuple-element.17), channel_id=1, source_target_pairs={{0,8},{8,16},{16,24},{1,9},{9,17},{17,25},{2,10},{10,18},{18,26},{... | collective-permute-start | bytes 294920 | tf_op jit(solution)/shard_map/ppermute | solution.py:28
  296.6 38.2 %copy-start.10 = (bf16[192,2,128]{2,0,1:T(8,128)(2,1)}, bf16[192,2,128]{2,0,1:T(8,128)(2,1)S(1)}, u32[]{:S(2)}) copy-start(bf16[192,2,128]{2,0,1:T(8,128)(2,1)S(1)} %get-tuple-element.15) | copy-start | bytes 294916
  320.6 7.4 %collective-permute-start.18 = (bf16[192,1,128]{2,0,1:T(8,128)(2,1)S(1)}, bf16[192,1,128]{2,0,1:T(8,128)(2,1)S(1)}, u32[]{:S(2)}, u32[]{:S(2)}) collective-permute-start(bf16[192,1,128]{2,0,1:T(8,128)(2,1)S(1)} %get-tuple-element.67), channel_id=1, source_target_pairs={{1,0},{2,1},{3,2},{4,3},{5,4},{6,5},{7,6},{9,8},{10,9},{11,10},{12... | collective-permute-start | bytes 147464 | tf_op jit(solution)/shard_map/ppermute | solution.py:20
  326.1 5.4 %collective-permute-start.17 = (bf16[192,1,128]{2,0,1:T(8,128)(2,1)S(1)}, bf16[192,1,128]{2,0,1:T(8,128)(2,1)S(1)}, u32[]{:S(2)}, u32[]{:S(2)}) collective-permute-start(bf16[192,1,128]{2,0,1:T(8,128)(2,1)S(1)} %get-tuple-element.66), channel_id=1, source_target_pairs={{0,1},{1,2},{2,3},{3,4},{4,5},{5,6},{6,7},{8,9},{9,10},{10,11},{11... | collective-permute-start | bytes 147464 | tf_op jit(solution)/shard_map/ppermute | solution.py:19
  359.9 7.9 %collective-permute-start.20 = (bf16[192,1,128]{2,0,1:T(8,128)(2,1)S(1)}, bf16[192,1,128]{2,0,1:T(8,128)(2,1)S(1)}, u32[]{:S(2)}, u32[]{:S(2)}) collective-permute-start(bf16[192,1,128]{2,0,1:T(8,128)(2,1)S(1)} %get-tuple-element.65), channel_id=1, source_target_pairs={{1,0},{2,1},{3,2},{4,3},{5,4},{6,5},{7,6},{9,8},{10,9},{11,10},{12... | collective-permute-start | bytes 147464 | tf_op jit(solution)/shard_map/ppermute | solution.py:20
  365.3 5.4 %collective-permute-start.19 = (bf16[192,1,128]{2,0,1:T(8,128)(2,1)S(1)}, bf16[192,1,128]{2,0,1:T(8,128)(2,1)S(1)}, u32[]{:S(2)}, u32[]{:S(2)}) collective-permute-start(bf16[192,1,128]{2,0,1:T(8,128)(2,1)S(1)} %get-tuple-element.64), channel_id=1, source_target_pairs={{0,1},{1,2},{2,3},{3,4},{4,5},{5,6},{6,7},{8,9},{9,10},{10,11},{11... | collective-permute-start | bytes 147464 | tf_op jit(solution)/shard_map/ppermute | solution.py:19
  367.7 7.2 %copy-start.7 = (bf16[576,1728]{1,0:T(8,128)(2,1)S(1)}, bf16[576,1728]{1,0:T(8,128)(2,1)}, u32[]{:S(2)}) copy-start(bf16[576,1728]{1,0:T(8,128)(2,1)} %reshape.216) | copy-start | bytes 5971972
  376.4 3.6 copy-start.36
  381.1 7.4 %collective-permute-start.21 = (bf16[192,2,128]{2,0,1:T(8,128)(2,1)S(1)}, bf16[192,2,128]{2,0,1:T(8,128)(2,1)S(1)}, u32[]{:S(2)}, u32[]{:S(2)}) collective-permute-start(bf16[192,2,128]{2,0,1:T(8,128)(2,1)S(1)} %get-tuple-element.11), channel_id=1, source_target_pairs={{0,8},{8,16},{16,24},{1,9},{9,17},{17,25},{2,10},{10,18},{18,26},{... | collective-permute-start | bytes 294920 | tf_op jit(solution)/shard_map/ppermute | solution.py:28
  383.1 5.5 %copy-start.24 = (bf16[9,192,2,128]{3,1,2,0:T(8,128)(2,1)}, bf16[9,192,2,128]{3,1,2,0:T(8,128)(2,1)S(1)}, u32[]{:S(2)}) copy-start(bf16[9,192,2,128]{3,1,2,0:T(8,128)(2,1)S(1)} %constant_dynamic-update-slice_fusion.85) | copy-start | bytes 2654212
  412.7 15.9 %copy-start.9 = (bf16[576,1728]{1,0:T(8,128)(2,1)S(1)}, bf16[576,1728]{1,0:T(8,128)(2,1)}, u32[]{:S(2)}) copy-start(bf16[576,1728]{1,0:T(8,128)(2,1)} %reshape.213) | copy-start | bytes 5971972
  413.7 8.7 %collective-permute-start.23 = (bf16[192,1,128]{2,0,1:T(8,128)(2,1)S(1)}, bf16[192,1,128]{2,0,1:T(8,128)(2,1)S(1)}, u32[]{:S(2)}, u32[]{:S(2)}) collective-permute-start(bf16[192,1,128]{2,0,1:T(8,128)(2,1)S(1)} %get-tuple-element.63), channel_id=1, source_target_pairs={{1,0},{2,1},{3,2},{4,3},{5,4},{6,5},{7,6},{9,8},{10,9},{11,10},{12... | collective-permute-start | bytes 147464 | tf_op jit(solution)/shard_map/ppermute | solution.py:20
  419.1 5.4 %collective-permute-start.22 = (bf16[192,1,128]{2,0,1:T(8,128)(2,1)S(1)}, bf16[192,1,128]{2,0,1:T(8,128)(2,1)S(1)}, u32[]{:S(2)}, u32[]{:S(2)}) collective-permute-start(bf16[192,1,128]{2,0,1:T(8,128)(2,1)S(1)} %get-tuple-element.62), channel_id=1, source_target_pairs={{0,1},{1,2},{2,3},{3,4},{4,5},{5,6},{6,7},{8,9},{9,10},{10,11},{11... | collective-permute-start | bytes 147464 | tf_op jit(solution)/shard_map/ppermute | solution.py:19
  458.9 12.0 %copy-start.25 = (bf16[9,192,2,128]{3,1,2,0:T(8,128)(2,1)S(1)}, bf16[9,192,2,128]{3,1,2,0:T(8,128)(2,1)}, u32[]{:S(2)}) copy-start(bf16[9,192,2,128]{3,1,2,0:T(8,128)(2,1)} %constant_dynamic-update-slice_fusion.84) | copy-start | bytes 2654212
  459.1 8.2 %collective-permute-start.25 = (bf16[192,1,128]{2,0,1:T(8,128)(2,1)S(1)}, bf16[192,1,128]{2,0,1:T(8,128)(2,1)S(1)}, u32[]{:S(2)}, u32[]{:S(2)}) collective-permute-start(bf16[192,1,128]{2,0,1:T(8,128)(2,1)S(1)} %get-tuple-element.61), channel_id=1, source_target_pairs={{1,0},{2,1},{3,2},{4,3},{5,4},{6,5},{7,6},{9,8},{10,9},{11,10},{12... | collective-permute-start | bytes 147464 | tf_op jit(solution)/shard_map/ppermute | solution.py:20
  464.7 5.4 %collective-permute-start.24 = (bf16[192,1,128]{2,0,1:T(8,128)(2,1)S(1)}, bf16[192,1,128]{2,0,1:T(8,128)(2,1)S(1)}, u32[]{:S(2)}, u32[]{:S(2)}) collective-permute-start(bf16[192,1,128]{2,0,1:T(8,128)(2,1)S(1)} %get-tuple-element.60), channel_id=1, source_target_pairs={{0,1},{1,2},{2,3},{3,4},{4,5},{5,6},{6,7},{8,9},{9,10},{10,11},{11... | collective-permute-start | bytes 147464 | tf_op jit(solution)/shard_map/ppermute | solution.py:19
  473.4 3.8 copy-start.31
  473.4 3.8 copy-start.32
  (17 other events, 28.8 us)
where the time goes:
time: 489 us; the launch traced here: 479 us
  blocking collectives  236 us (48%)
  starting transfers between devices  88.6 us (18%)
  local copies, waits for them, and re-layouts  73.4 us (15%)
  waiting for transfers between devices  44.1 us (9%)
  other arithmetic  19.7 us (4%)
  matrix products  14.2 us (3%)
    psum x10, blocking collectives, activate(): lax.psum(jnp.sum(centred * centred, axis=(1, 2, 3)), 'rows') / cell_count  130 us
    psum x10, blocking collectives, activate(): average = lax.psum(jnp.sum(grouped, axis=(1, 2, 3)), 'rows') / cell_count  106 us
    ppermute x11, starting transfers between devices, with_halo(): after = lax.ppermute(leading, axis, down)  56.6 us
    ppermute x11, waiting for transfers between devices, with_halo(): before = lax.ppermute(last, axis, up)  25.6 us
    ppermute x11, starting transfers between devices, with_halo(): before = lax.ppermute(last, axis, up)  22.3 us
    ppermute x4, waiting for transfers between devices, passed_along(): lax.ppermute(value, axis, [(source, source + steps) for source in range(l...  18.5 us
    unnamed x181, local copies, waits for them, and re-layouts  14.8 us
    dot_general x10, matrix products, causal_conv(): running = jnp.dot(taps, stacked, preferred_element_type=jnp.float32)  14.2 us
  transfers between devices with their start and end apart: 26, of which 13 were waited for; matrix products, arithmetic and copies ran while one was open for 7% of the time, Pallas kernels for 0%

commit v1 on v0

v1 whole, which is shorter than its diff:
```python
import jax
import jax.numpy as jnp
from jax import lax
from jax.sharding import PartitionSpec as P

GROUPS = 32
EPS = 1e-06
MAX_SPAN = 16


def span_devices(peers, rows_here):
    count = 1
    while count * 2 <= peers and peers % (count * 2) == 0 and count * 2 * rows_here <= MAX_SPAN:
        count *= 2
    return count


def gather_span(array, dim, span_count):
    if span_count == 1:
        return array
    peers = lax.axis_size("rows")
    if span_count == peers:
        return lax.all_gather(array, "rows", axis=dim, tiled=True)
    place = lax.axis_index("rows") % span_count
    pieces = [array]
    for shift in range(1, span_count):
        pairs = [
            (b * span_count + p, b * span_count + (p + shift) % span_count)
            for b in range(peers // span_count)
            for p in range(span_count)
        ]
        pieces.append(lax.ppermute(array, "rows", pairs))
    stacked = jnp.stack(pieces)
    order = (place - jnp.arange(span_count)) % span_count
    picked = jnp.take(stacked, order, axis=0)
    picked = jnp.moveaxis(picked, 0, dim)
    shape = list(array.shape)
    shape[dim] = shape[dim] * span_count
    return picked.reshape(shape)


def with_rim(array, dim, span_count):
    peers = lax.axis_size("rows")
    length = array.shape[dim]
    if span_count == peers:
        pad = [(0, 0)] * array.ndim
        pad[dim] = (1, 1)
        return jnp.pad(array, pad)
    up = [(i, i + span_count) for i in range(peers - span_count)]
    down = [(j, i) for i, j in up]
    last = lax.slice_in_dim(array, length - 1, length, axis=dim)
    leading = lax.slice_in_dim(array, 0, 1, axis=dim)
    before = lax.ppermute(last, "rows", up)
    after = lax.ppermute(leading, "rows", down)
    return jnp.concatenate([before, array, after], axis=dim)


def arrange_taps(weight):
    outputs = weight.shape[3]
    channels = weight.shape[4]
    return jnp.transpose(weight, (2, 3, 0, 1, 4)).reshape(3 * outputs, 9 * channels)


def causal_conv(window, taps, rows_out):
    channels = window.shape[1]
    columns = window.shape[3]
    outputs = taps.shape[0] // 3
    pieces = [
        window[step_t, :, step_y : step_y + rows_out, :]
        for step_t in range(3)
        for step_y in range(3)
    ]
    stacked = jnp.stack(pieces).reshape(9 * channels, rows_out * columns)
    running = jnp.dot(taps, stacked, preferred_element_type=jnp.float32)
    running = running.reshape(3, outputs, rows_out, columns)
    leftward = jnp.pad(running[0, :, :, :-1], ((0, 0), (0, 0), (1, 0)))
    rightward = jnp.pad(running[2, :, :, 1:], ((0, 0), (0, 0), (0, 1)))
    return running[1] + leftward + rightward


def block_sum(values, span_count):
    peers = lax.axis_size("rows")
    if span_count == peers:
        return values
    lead = (lax.axis_index("rows") % span_count == 0).astype(values.dtype)
    return lax.psum(values * lead, "rows")


def activate(source, gain_vec, shift_vec, cell_count, span_count):
    channels, height, columns = source.shape
    grouped = source.astype(jnp.float32).reshape(GROUPS, channels // GROUPS, height, columns)
    average = block_sum(jnp.sum(grouped, axis=(1, 2, 3)), span_count) / cell_count
    centred = grouped - average[:, None, None, None]
    spread = block_sum(jnp.sum(centred * centred, axis=(1, 2, 3)), span_count) / cell_count
    inverse = lax.rsqrt(spread + EPS)
    normed = (centred * inverse[:, None, None, None]).reshape(channels, height, columns)
    normed = normed * gain_vec[:, None, None] + shift_vec[:, None, None]
    return jax.nn.silu(normed).astype(jnp.bfloat16)


def run_frame(source, first_hist, second_hist, kernels, biases, gains, shifts, cell_count, span_count):
    span = source.shape[1]
    first_in = with_rim(activate(source, gains[0], shifts[0], cell_count, span_count), 1, span_count)
    first_win = jnp.concatenate([first_hist, first_in[None]], axis=0)
    hidden = (causal_conv(first_win, kernels[0], span) + biases[0][:, None, None]).astype(jnp.bfloat16)
    second_in = with_rim(activate(hidden, gains[1], shifts[1], cell_count, span_count), 1, span_count)
    second_win = jnp.concatenate([second_hist, second_in[None]], axis=0)
    result = causal_conv(second_win, kernels[1], span) + biases[1][:, None, None] + source.astype(jnp.float32)
    return (result.astype(jnp.bfloat16), first_win[1:], second_win[1:])


def shards(frames, causal_cache, conv_weight, conv_bias, norm_gain, norm_shift):
    phase_no = lax.axis_index("phase")
    phase_count = lax.axis_size("phase")
    peers = lax.axis_size("rows")
    frame_count = frames.shape[0]
    channels = frames.shape[1]
    rows_here = frames.shape[2]
    columns = frames.shape[3]
    span_count = span_devices(peers, rows_here)
    span = rows_here * span_count
    cell_count = float(channels // GROUPS * rows_here * peers * columns)
    frames_span = gather_span(frames, 2, span_count)
    cache_span = gather_span(causal_cache[0], 3, span_count)
    rimmed = with_rim(cache_span, 3, span_count)
    first_hist = rimmed[0]
    second_hist = rimmed[1]
    local_taps = (arrange_taps(conv_weight[0, 0]), arrange_taps(conv_weight[0, 1]))
    incoming = jnp.zeros_like(frames_span[0])
    produced = jnp.zeros_like(frames_span)
    tick_count = frame_count + phase_count - 1
    for tick_no in range(tick_count):
        frame_no = tick_no - phase_no
        active_now = jnp.logical_and(frame_no >= 0, frame_no < frame_count)
        source = jnp.where(phase_no == 0, frames_span[min(tick_no, frame_count - 1)], incoming)
        result, first_next, second_next = run_frame(
            source, first_hist, second_hist, local_taps, conv_bias[0], norm_gain[0], norm_shift[0],
            cell_count, span_count,
        )
        first_hist = jnp.where(active_now, first_next, first_hist)
        second_hist = jnp.where(active_now, second_next, second_hist)
        frame_slot = jnp.clip(frame_no, 0, frame_count - 1)
        produced = jnp.where(
            active_now, lax.dynamic_update_index_in_dim(produced, result, frame_slot, 0), produced
        )
        if tick_no + 1 < tick_count:
            incoming = lax.ppermute(result, "phase", [(s, s + 1) for s in range(phase_count - 1)])
    start = (lax.axis_index("rows") % span_count) * rows_here
    new_cache = jnp.stack([first_hist[:, :, 1 : 1 + span, :], second_hist[:, :, 1 : 1 + span, :]])
    produced = lax.dynamic_slice_in_dim(produced, start, rows_here, axis=2)
    new_cache = lax.dynamic_slice_in_dim(new_cache, start, rows_here, axis=3)
    return (produced[None], new_cache[None])


def solution(mesh):
    in_specs = (
        P(None, None, "rows", None),
        P("phase", None, None, None, "rows", None),
        P("phase", None, None, None, None, None, None),
        P("phase", None, None),
        P("phase", None, None),
        P("phase", None, None),
    )
    out_specs = (P("phase", None, None, "rows", None), P("phase", None, None, None, "rows", None))
    return jax.shard_map(shards, mesh=mesh, in_specs=in_specs, out_specs=out_specs, check_vma=False)
```

time: 489 us -> 442 us (0.904)
  the two profiles are of different devices: /device:TPU:12 before, /device:TPU:4 now
where the time goes in v1:
time: 442 us; the launch traced here: 438 us
  local copies, waits for them, and re-layouts  197 us (45%)
  waiting for transfers between devices  97.8 us (22%)
  other arithmetic  60.2 us (14%)
  matrix products  55.6 us (13%)
  between operations  16.8 us (4%)
  starting transfers between devices  9.77 us (2%)
    another operation x20, local copies, waits for them, and re-layouts, causal_conv(): stacked = jnp.stack(pieces).reshape(9 * channels, rows_out * columns)  83 us
    unnamed x266, local copies, waits for them, and re-layouts  66.5 us
    ppermute x4, waiting for transfers between devices, shards(): lax.ppermute(result, 'phase', [(s, s + 1) for s in range(phase_count - 1)])  59.6 us
    dot_general x10, matrix products, causal_conv(): running = jnp.dot(taps, stacked, preferred_element_type=jnp.float32)  55.6 us
    all_gather x2, waiting for transfers between devices, gather_span(): return lax.all_gather(array, 'rows', axis=dim, tiled=True)  38.2 us
    reduce_sum x20, other arithmetic, activate(): jnp.sum(grouped, axis=(1, 2, 3))  14.9 us
    reduce_sum x20, other arithmetic, activate(): jnp.sum(centred * centred, axis=(1, 2, 3))  14.7 us
    convert_element_type x10, other arithmetic, activate(): return jax.nn.silu(normed).astype(jnp.bfloat16)  14.4 us
  transfers between devices with their start and end apart: 6, of which 6 were waited for; matrix products, arithmetic and copies ran while one was open for 8% of the time, Pallas kernels for 0%

profile of v1, /device:TPU:4, one launch (start us, length us, event | category | flops | bytes accessed | tf_op | source)
XLA Modules:
  0.0 437.6 jit_solution(14004337137466954886)
XLA Ops:
  10.8 4.7 %slice_bitcast_fusion.1 = (bf16[3,192,3,3,192]{4,1,0,3,2:T(8,128)(2,1)S(1)}, bf16[3,192,3,3,192]{4,1,0,3,2:T(8,128)(2,1)}) fusion(bf16[1,2,3,3,3,192,192]{6,5,4,3,2,1,0:T(8,128)(2,1)} %param.8), kind=kLoop, calls=%fused_computation.36 | loop fusion | bytes 7962624 | tf_op jit(solution)/shard_map/transpose | solution.py:61
  15.5 2.3 copy.92
  17.8 4.5 %reshape.267 = bf16[576,1728]{1,0:T(8,128)(2,1)} reshape(bf16[3,192,3,3,192]{4,3,2,1,0:T(4,128)(2,1)S(1)} %copy.92) | data formatting | bytes 3981312 | tf_op jit(solution)/shard_map/reshape | solution.py:61
  22.2 4.0 copy.97
  26.3 4.2 reshape.270
  32.4 4.2 all-gather.4.cloned.1.call-done
  42.5 34.0 %all-gather.6.cloned.1.call-done = bf16[1,2,2,192,16,128]{5,3,2,1,0,4:T(8,128)(2,1)} async-done(((bf16[1,2,2,192,2,128]{5,3,2,1,0,4:T(8,128)(2,1)}), bf16[1,2,2,192,16,128]{5,3,2,1,0,4:T(8,128)(2,1)}) %all-gather.6.cloned.1.call-update) | async-done | bytes 3145744 | tf_op jit(solution)/shard_map/all_gather | solution.py:23
  76.6 2.1 copy.274
  81.4 8.0 %copy.91 = bf16[9,192,16,128]{3,2,1,0:T(8,128)(2,1)} copy(bf16[9,192,16,128]{3,1,2,0:T(8,128)(2,1)S(1)} %slice_dynamic-update-slice_fusion.75) | data formatting | bytes 14155776 | tf_op jit(solution)/shard_map/stack | solution.py:73
  89.3 7.2 %fusion.27 = f32[2048,576]{0,1:T(8,128)S(1)} fusion(bf16[576,1728]{1,0:T(8,128)(2,1)S(1)} %copy-done.47, bf16[216,8,16,128]{3,2,1,0:T(8,128)(2,1)} %bitcast.445), kind=kOutput, calls=%fused_computation.27 | convolution fusion | flops 4076863488 | bytes 13787136 | tf_op jit(solution)/shard_map/dot_general | solution.py:74
  99.2 2.0 convert_reduce_fusion.9
  104.0 2.0 fusion.132
  108.9 2.1 fusion.140
  112.0 8.0 %copy.96 = bf16[9,192,16,128]{3,2,1,0:T(8,128)(2,1)} copy(bf16[9,192,16,128]{3,1,2,0:T(8,128)(2,1)S(1)} %slice_dynamic-update-slice_fusion.72) | data formatting | bytes 14155776 | tf_op jit(solution)/shard_map/stack | solution.py:73
  120.0 6.9 %fusion.24 = f32[2048,576]{0,1:T(8,128)S(1)} fusion(bf16[576,1728]{1,0:T(8,128)(2,1)S(1)} %copy-done.43, bf16[216,8,16,128]{3,2,1,0:T(8,128)(2,1)} %bitcast.446), kind=kOutput, calls=%fused_computation.24 | convolution fusion | flops 4076863488 | bytes 13787136 | tf_op jit(solution)/shard_map/dot_general | solution.py:74
  133.4 3.4 collective-permute-start
  138.1 2.3 copy-done.33
  140.4 15.5 %collective-permute-done = bf16[192,16,128]{2,0,1:T(8,128)(2,1)S(1)} collective-permute-done((bf16[192,16,128]{2,0,1:T(8,128)(2,1)S(1)}, bf16[192,16,128]{2,0,1:T(8,128)(2,1)S(1)}, u32[]{:S(2)}, u32[]{:S(2)}) %collective-permute-start) | collective-permute-done | bytes 786464 | tf_op jit(solution)/shard_map/ppermute | solution.py:147
  161.5 8.0 %copy.102 = bf16[9,192,16,128]{3,2,1,0:T(8,128)(2,1)S(1)} copy(bf16[9,192,16,128]{3,1,2,0:T(8,128)(2,1)} %slice_dynamic-update-slice_fusion.57) | data formatting | bytes 14155776 | tf_op jit(solution)/shard_map/stack | solution.py:73
  169.5 4.8 %fusion.21 = f32[2048,576]{0,1:T(8,128)S(1)} fusion(bf16[576,1728]{1,0:T(8,128)(2,1)S(1)} %copy-done.48, bf16[216,8,16,128]{3,2,1,0:T(8,128)(2,1)S(1)} %bitcast.447), kind=kOutput, calls=%fused_computation.21 | convolution fusion | flops 4076863488 | bytes 13787136 | tf_op jit(solution)/shard_map/dot_general | solution.py:74
  184.9 8.0 %copy.106 = bf16[9,192,16,128]{3,2,1,0:T(8,128)(2,1)S(1)} copy(bf16[9,192,16,128]{3,1,2,0:T(8,128)(2,1)} %slice_dynamic-update-slice_fusion.54) | data formatting | bytes 14155776 | tf_op jit(solution)/shard_map/stack | solution.py:73
  192.9 4.6 %fusion.18 = f32[2048,576]{0,1:T(8,128)S(1)} fusion(bf16[576,1728]{1,0:T(8,128)(2,1)S(1)} %copy-done.44, bf16[216,8,16,128]{3,2,1,0:T(8,128)(2,1)S(1)} %bitcast.448), kind=kOutput, calls=%fused_computation.18 | convolution fusion | flops 4076863488 | bytes 13787136 | tf_op jit(solution)/shard_map/dot_general | solution.py:74
  202.3 2.5 collective-permute-start.1
  205.7 2.6 copy-done.35
  208.7 15.3 %collective-permute-done.1 = bf16[192,16,128]{2,0,1:T(8,128)(2,1)S(1)} collective-permute-done((bf16[192,16,128]{2,0,1:T(8,128)(2,1)S(1)}, bf16[192,16,128]{2,0,1:T(8,128)(2,1)S(1)}, u32[]{:S(2)}, u32[]{:S(2)}) %collective-permute-start.1) | collective-permute-done | bytes 786464 | tf_op jit(solution)/shard_map/ppermute | solution.py:147
  228.6 2.0 fusion.78
  233.4 2.1 fusion.86
  238.6 8.0 %copy.110 = bf16[9,192,16,128]{3,2,1,0:T(8,128)(2,1)S(1)} copy(bf16[9,192,16,128]{3,1,2,0:T(8,128)(2,1)} %slice_dynamic-update-slice_fusion.39) | data formatting | bytes 14155776 | tf_op jit(solution)/shard_map/stack | solution.py:73
  246.6 4.8 %fusion.15 = f32[2048,576]{0,1:T(8,128)S(1)} fusion(bf16[576,1728]{1,0:T(8,128)(2,1)S(1)} %copy-done.49, bf16[216,8,16,128]{3,2,1,0:T(8,128)(2,1)S(1)} %bitcast.449), kind=kOutput, calls=%fused_computation.15 | convolution fusion | flops 4076863488 | bytes 13787136 | tf_op jit(solution)/shard_map/dot_general | solution.py:74
  259.0 2.0 fusion.114
  263.9 2.2 fusion.122
  269.9 8.0 %copy.114 = bf16[9,192,16,128]{3,2,1,0:T(8,128)(2,1)S(1)} copy(bf16[9,192,16,128]{3,1,2,0:T(8,128)(2,1)} %slice_dynamic-update-slice_fusion.36) | data formatting | bytes 14155776 | tf_op jit(solution)/shard_map/stack | solution.py:73
  277.9 4.6 %fusion.12 = f32[2048,576]{0,1:T(8,128)S(1)} fusion(bf16[576,1728]{1,0:T(8,128)(2,1)S(1)} %copy-done.45, bf16[216,8,16,128]{3,2,1,0:T(8,128)(2,1)S(1)} %bitcast.450), kind=kOutput, calls=%fused_computation.12 | convolution fusion | flops 4076863488 | bytes 13787136 | tf_op jit(solution)/shard_map/dot_general | solution.py:74
  290.2 2.6 copy-done.37
  293.2 14.8 %collective-permute-done.2 = bf16[192,16,128]{2,0,1:T(8,128)(2,1)S(1)} collective-permute-done((bf16[192,16,128]{2,0,1:T(8,128)(2,1)S(1)}, bf16[192,16,128]{2,0,1:T(8,128)(2,1)S(1)}, u32[]{:S(2)}, u32[]{:S(2)}) %collective-permute-start.2) | collective-permute-done | bytes 786464 | tf_op jit(solution)/shard_map/ppermute | solution.py:147
  313.7 8.0 %copy.118 = bf16[9,192,16,128]{3,2,1,0:T(8,128)(2,1)S(1)} copy(bf16[9,192,16,128]{3,1,2,0:T(8,128)(2,1)} %slice_dynamic-update-slice_fusion.21) | data formatting | bytes 14155776 | tf_op jit(solution)/shard_map/stack | solution.py:73
  321.7 4.8 %fusion.9 = f32[2048,576]{0,1:T(8,128)S(1)} fusion(bf16[576,1728]{1,0:T(8,128)(2,1)S(1)} %copy-done.50, bf16[216,8,16,128]{3,2,1,0:T(8,128)(2,1)S(1)} %bitcast.451), kind=kOutput, calls=%fused_computation.9 | convolution fusion | flops 4076863488 | bytes 13787136 | tf_op jit(solution)/shard_map/dot_general | solution.py:74
  337.1 8.0 %copy.122 = bf16[9,192,16,128]{3,2,1,0:T(8,128)(2,1)S(1)} copy(bf16[9,192,16,128]{3,1,2,0:T(8,128)(2,1)} %slice_dynamic-update-slice_fusion.18) | data formatting | bytes 14155776 | tf_op jit(solution)/shard_map/stack | solution.py:73
  345.1 4.6 %fusion.6 = f32[2048,576]{0,1:T(8,128)S(1)} fusion(bf16[576,1728]{1,0:T(8,128)(2,1)S(1)} %copy-done.46, bf16[216,8,16,128]{3,2,1,0:T(8,128)(2,1)S(1)} %bitcast.452), kind=kOutput, calls=%fused_computation.6 | convolution fusion | flops 4076863488 | bytes 13787136 | tf_op jit(solution)/shard_map/dot_general | solution.py:74
  357.3 2.6 copy-done.39
  360.3 14.0 %collective-permute-done.3 = bf16[192,16,128]{2,0,1:T(8,128)(2,1)S(1)} collective-permute-done((bf16[192,16,128]{2,0,1:T(8,128)(2,1)S(1)}, bf16[192,16,128]{2,0,1:T(8,128)(2,1)S(1)}, u32[]{:S(2)}, u32[]{:S(2)}) %collective-permute-start.3) | collective-permute-done | bytes 786464 | tf_op jit(solution)/shard_map/ppermute | solution.py:147
  378.9 2.0 fusion.60
  383.7 2.1 fusion.68
  387.3 2.1 copy-done.40
  389.8 8.0 %copy.126 = bf16[9,192,16,128]{3,2,1,0:T(8,128)(2,1)} copy(bf16[9,192,16,128]{3,1,2,0:T(8,128)(2,1)S(1)} %slice_dynamic-update-slice_fusion.3) | data formatting | bytes 14155776 | tf_op jit(solution)/shard_map/stack | solution.py:73
  397.8 7.0 %fusion.3 = f32[2048,576]{0,1:T(8,128)S(1)} fusion(bf16[576,1728]{1,0:T(8,128)(2,1)S(1)} %copy-done.51, bf16[216,8,16,128]{3,2,1,0:T(8,128)(2,1)} %bitcast.443), kind=kOutput, calls=%fused_computation.3 | convolution fusion | flops 4076863488 | bytes 13787136 | tf_op jit(solution)/shard_map/dot_general | solution.py:74
  413.6 4.9 %copy.130 = bf16[9,192,16,128]{3,2,1,0:T(8,128)(2,1)S(1)} copy(bf16[9,192,16,128]{3,1,2,0:T(8,128)(2,1)S(1)} %slice_dynamic-update-slice_fusion) | data formatting | bytes 14155776 | tf_op jit(solution)/shard_map/stack | solution.py:73
  418.5 6.3 %fusion = f32[2048,576]{0,1:T(8,128)S(1)} fusion(bf16[576,1728]{1,0:T(8,128)(2,1)} %reshape.270, bf16[216,8,16,128]{3,2,1,0:T(8,128)(2,1)S(1)} %bitcast.444), kind=kOutput, calls=%fused_computation | convolution fusion | flops 4076863488 | bytes 13787136 | tf_op jit(solution)/shard_map/dot_general | solution.py:74
  (441 shorter events, 131.6 us)
Async XLA Ops:
  7.2 29.4 %all-gather.4.cloned.1.call-start = ((), (), s32[]{:S(2)}) async-start(), calls=%async_computation | async-start | bytes 1769472 | tf_op jit(solution)/shard_map/all_gather | solution.py:23
  8.9 67.7 %all-gather.6.cloned.1.call-start = ((), (), s32[]{:S(2)}) async-start(), calls=%async_computation.1 | async-start | bytes 3538944 | tf_op jit(solution)/shard_map/all_gather | solution.py:23
  26.3 4.3 copy-start.72
  26.3 4.9 %copy-start.73 = (f32[1,2,192]{2,1,0:T(2,128)S(1)}, f32[1,2,192]{2,1,0:T(2,128)}, u32[]{:S(2)}) copy-start(f32[1,2,192]{2,1,0:T(2,128)} %param.11) | copy-start | bytes 4612
  26.3 5.4 %copy-start.74 = (f32[1,2,192]{2,1,0:T(2,128)S(1)}, f32[1,2,192]{2,1,0:T(2,128)}, u32[]{:S(2)}) copy-start(f32[1,2,192]{2,1,0:T(2,128)} %param.9) | copy-start | bytes 4612
  31.2 11.4 %copy-start.66 = (f32[1,1,192]{2,1,0:T(1,128)}, f32[1,1,192]{2,1,0:T(1,128)S(1)}, u32[]{:S(2)}) copy-start(f32[1,1,192]{2,1,0:T(1,128)S(1)} %get-tuple-element.55) | copy-start | bytes 2308
  31.8 10.8 %copy-start.69 = (f32[1,1,192]{2,1,0:T(1,128)}, f32[1,1,192]{2,1,0:T(1,128)S(1)}, u32[]{:S(2)}) copy-start(f32[1,1,192]{2,1,0:T(1,128)S(1)} %get-tuple-element.57) | copy-start | bytes 2308
  32.4 66.8 %copy-start.61 = (f32[1,1,192]{2,1,0:T(1,128)}, f32[1,1,192]{2,1,0:T(1,128)S(1)}, u32[]{:S(2)}) copy-start(f32[1,1,192]{2,1,0:T(1,128)S(1)} %get-tuple-element.58) | copy-start | bytes 2308
  36.5 3.9 copy-start.8
  79.2 32.4 %copy-start.6 = (bf16[2,192,18,128]{3,1,2,0:T(8,128)(2,1)}, bf16[2,192,18,128]{3,1,2,0:T(8,128)(2,1)S(1)}, u32[]{:S(2)}) copy-start(bf16[2,192,18,128]{3,1,2,0:T(8,128)(2,1)S(1)} %get-tuple-element.53) | copy-start | bytes 5308420
  81.4 8.0 %copy-start.47 = (bf16[576,1728]{1,0:T(8,128)(2,1)S(1)}, bf16[576,1728]{1,0:T(8,128)(2,1)}, u32[]{:S(2)}) copy-start(bf16[576,1728]{1,0:T(8,128)(2,1)} %reshape.267) | copy-start | bytes 5971972
  112.0 8.0 %copy-start.43 = (bf16[576,1728]{1,0:T(8,128)(2,1)S(1)}, bf16[576,1728]{1,0:T(8,128)(2,1)}, u32[]{:S(2)}) copy-start(bf16[576,1728]{1,0:T(8,128)(2,1)} %reshape.270) | copy-start | bytes 5971972
  130.1 7.9 %copy-start.4 = (bf16[2,192,18,128]{3,1,2,0:T(8,128)(2,1)}, bf16[2,192,18,128]{3,1,2,0:T(8,128)(2,1)S(1)}, u32[]{:S(2)}) copy-start(bf16[2,192,18,128]{3,1,2,0:T(8,128)(2,1)S(1)} %get-tuple-element.61) | copy-start | bytes 5308420
  133.4 3.7 copy-start.19
  133.4 22.5 %collective-permute-start = (bf16[192,16,128]{2,0,1:T(8,128)(2,1)S(1)}, bf16[192,16,128]{2,0,1:T(8,128)(2,1)S(1)}, u32[]{:S(2)}, u32[]{:S(2)}) collective-permute-start(bf16[192,16,128]{2,0,1:T(8,128)(2,1)S(1)} %get-tuple-element.27), channel_id=1, source_target_pairs={{0,8},{8,16},{16,24},{1,9},{9,17},{17,25},{2,10},{10,18},{18,26},{... | collective-permute-start | bytes 2359304 | tf_op jit(solution)/shard_map/ppermute | solution.py:147
  137.4 2.9 copy-start.33
  140.4 15.9 %copy-start.34 = (bf16[9,192,16,128]{3,1,2,0:T(8,128)(2,1)}, bf16[9,192,16,128]{3,1,2,0:T(8,128)(2,1)S(1)}, u32[]{:S(2)}) copy-start(bf16[9,192,16,128]{3,1,2,0:T(8,128)(2,1)S(1)} %slice_dynamic-update-slice_fusion.66) | copy-start | bytes 21233668
  140.4 17.1 %copy-start.67 = (f32[1,1,192]{2,1,0:T(1,128)S(1)}, f32[1,1,192]{2,1,0:T(1,128)}, u32[]{:S(2)}) copy-start(f32[1,1,192]{2,1,0:T(1,128)} %copy-done.66) | copy-start | bytes 2308
  140.4 17.1 %copy-start.70 = (f32[1,1,192]{2,1,0:T(1,128)S(1)}, f32[1,1,192]{2,1,0:T(1,128)}, u32[]{:S(2)}) copy-start(f32[1,1,192]{2,1,0:T(1,128)} %copy-done.69) | copy-start | bytes 2308
  156.2 2.3 copy-start.27
  161.5 8.0 %copy-start.48 = (bf16[576,1728]{1,0:T(8,128)(2,1)S(1)}, bf16[576,1728]{1,0:T(8,128)(2,1)}, u32[]{:S(2)}) copy-start(bf16[576,1728]{1,0:T(8,128)(2,1)} %reshape.267) | copy-start | bytes 5971972
  184.9 8.0 %copy-start.44 = (bf16[576,1728]{1,0:T(8,128)(2,1)S(1)}, bf16[576,1728]{1,0:T(8,128)(2,1)}, u32[]{:S(2)}) copy-start(bf16[576,1728]{1,0:T(8,128)(2,1)} %reshape.270) | copy-start | bytes 5971972
  202.3 2.8 copy-start.21
  202.3 21.7 %collective-permute-start.1 = (bf16[192,16,128]{2,0,1:T(8,128)(2,1)S(1)}, bf16[192,16,128]{2,0,1:T(8,128)(2,1)S(1)}, u32[]{:S(2)}, u32[]{:S(2)}) collective-permute-start(bf16[192,16,128]{2,0,1:T(8,128)(2,1)S(1)} %get-tuple-element.21), channel_id=1, source_target_pairs={{0,8},{8,16},{16,24},{1,9},{9,17},{17,25},{2,10},{10,18},{18,26},{... | collective-permute-start | bytes 2359304 | tf_op jit(solution)/shard_map/ppermute | solution.py:147
  205.4 2.9 copy-start.35
  208.4 15.5 %copy-start.10 = (bf16[2,192,16,128]{3,1,0,2:T(8,128)(2,1)S(1)}, bf16[2,192,16,128]{3,1,0,2:T(8,128)(2,1)}, u32[]{:S(2)}) copy-start(bf16[2,192,16,128]{3,1,0,2:T(8,128)(2,1)} %all-gather.4.cloned.1.call-done) | copy-start | bytes 4718596
  208.7 17.1 %copy-start.36 = (bf16[9,192,16,128]{3,1,2,0:T(8,128)(2,1)}, bf16[9,192,16,128]{3,1,2,0:T(8,128)(2,1)S(1)}, u32[]{:S(2)}) copy-start(bf16[9,192,16,128]{3,1,2,0:T(8,128)(2,1)S(1)} %slice_dynamic-update-slice_fusion.48) | copy-start | bytes 21233668
  238.6 8.0 %copy-start.49 = (bf16[576,1728]{1,0:T(8,128)(2,1)S(1)}, bf16[576,1728]{1,0:T(8,128)(2,1)}, u32[]{:S(2)}) copy-start(bf16[576,1728]{1,0:T(8,128)(2,1)} %reshape.267) | copy-start | bytes 5971972
  263.9 2.3 copy-start.17
  266.5 23.3 %copy-start = (bf16[2,192,18,128]{3,1,2,0:T(8,128)(2,1)}, bf16[2,192,18,128]{3,1,2,0:T(8,128)(2,1)S(1)}, u32[]{:S(2)}) copy-start(bf16[2,192,18,128]{3,1,2,0:T(8,128)(2,1)S(1)} %fusion.54) | copy-start | bytes 5308420
  266.7 26.3 %copy-start.2 = (bf16[2,192,18,128]{3,1,2,0:T(8,128)(2,1)}, bf16[2,192,18,128]{3,1,2,0:T(8,128)(2,1)S(1)}, u32[]{:S(2)}) copy-start(bf16[2,192,18,128]{3,1,2,0:T(8,128)(2,1)S(1)} %fusion.55) | copy-start | bytes 5308420
  269.9 8.0 %copy-start.45 = (bf16[576,1728]{1,0:T(8,128)(2,1)S(1)}, bf16[576,1728]{1,0:T(8,128)(2,1)}, u32[]{:S(2)}) copy-start(bf16[576,1728]{1,0:T(8,128)(2,1)} %reshape.270) | copy-start | bytes 5971972
  287.3 20.7 %collective-permute-start.2 = (bf16[192,16,128]{2,0,1:T(8,128)(2,1)S(1)}, bf16[192,16,128]{2,0,1:T(8,128)(2,1)S(1)}, u32[]{:S(2)}, u32[]{:S(2)}) collective-permute-start(bf16[192,16,128]{2,0,1:T(8,128)(2,1)S(1)} %get-tuple-element.15), channel_id=1, source_target_pairs={{0,8},{8,16},{16,24},{1,9},{9,17},{17,25},{2,10},{10,18},{18,26},{... | collective-permute-start | bytes 2359304 | tf_op jit(solution)/shard_map/ppermute | solution.py:147
  289.9 2.9 copy-start.37
  292.9 15.1 %copy-start.11 = (bf16[2,192,16,128]{3,1,0,2:T(8,128)(2,1)S(1)}, bf16[2,192,16,128]{3,1,0,2:T(8,128)(2,1)}, u32[]{:S(2)}) copy-start(bf16[2,192,16,128]{3,1,0,2:T(8,128)(2,1)} %all-gather.4.cloned.1.call-done) | copy-start | bytes 4718596
  293.2 15.2 %copy-start.38 = (bf16[9,192,16,128]{3,1,2,0:T(8,128)(2,1)}, bf16[9,192,16,128]{3,1,2,0:T(8,128)(2,1)S(1)}, u32[]{:S(2)}) copy-start(bf16[9,192,16,128]{3,1,2,0:T(8,128)(2,1)S(1)} %slice_dynamic-update-slice_fusion.30) | copy-start | bytes 21233668
  293.2 16.4 %copy-start.68 = (f32[1,1,192]{2,1,0:T(1,128)S(1)}, f32[1,1,192]{2,1,0:T(1,128)}, u32[]{:S(2)}) copy-start(f32[1,1,192]{2,1,0:T(1,128)} %copy-done.66) | copy-start | bytes 2308
  293.2 16.4 %copy-start.71 = (f32[1,1,192]{2,1,0:T(1,128)S(1)}, f32[1,1,192]{2,1,0:T(1,128)}, u32[]{:S(2)}) copy-start(f32[1,1,192]{2,1,0:T(1,128)} %copy-done.69) | copy-start | bytes 2308
  313.7 8.0 %copy-start.50 = (bf16[576,1728]{1,0:T(8,128)(2,1)S(1)}, bf16[576,1728]{1,0:T(8,128)(2,1)}, u32[]{:S(2)}) copy-start(bf16[576,1728]{1,0:T(8,128)(2,1)} %reshape.267) | copy-start | bytes 5971972
  337.1 8.0 %copy-start.46 = (bf16[576,1728]{1,0:T(8,128)(2,1)S(1)}, bf16[576,1728]{1,0:T(8,128)(2,1)}, u32[]{:S(2)}) copy-start(bf16[576,1728]{1,0:T(8,128)(2,1)} %reshape.270) | copy-start | bytes 5971972
  354.5 19.8 %collective-permute-start.3 = (bf16[192,16,128]{2,0,1:T(8,128)(2,1)S(1)}, bf16[192,16,128]{2,0,1:T(8,128)(2,1)S(1)}, u32[]{:S(2)}, u32[]{:S(2)}) collective-permute-start(bf16[192,16,128]{2,0,1:T(8,128)(2,1)S(1)} %get-tuple-element.9), channel_id=1, source_target_pairs={{0,8},{8,16},{16,24},{1,9},{9,17},{17,25},{2,10},{10,18},{18,26},{... | collective-permute-start | bytes 2359304 | tf_op jit(solution)/shard_map/ppermute | solution.py:147
  357.1 2.9 copy-start.39
  360.1 14.2 %copy-start.12 = (bf16[2,192,16,128]{3,1,0,2:T(8,128)(2,1)S(1)}, bf16[2,192,16,128]{3,1,0,2:T(8,128)(2,1)}, u32[]{:S(2)}) copy-start(bf16[2,192,16,128]{3,1,0,2:T(8,128)(2,1)} %all-gather.4.cloned.1.call-done) | copy-start | bytes 4718596
  360.3 15.7 %copy-start.41 = (bf16[9,192,16,128]{3,1,2,0:T(8,128)(2,1)}, bf16[9,192,16,128]{3,1,2,0:T(8,128)(2,1)S(1)}, u32[]{:S(2)}) copy-start(bf16[9,192,16,128]{3,1,2,0:T(8,128)(2,1)S(1)} %slice_dynamic-update-slice_fusion.12) | copy-start | bytes 21233668
  385.9 3.6 copy-start.40
  389.8 8.0 %copy-start.51 = (bf16[576,1728]{1,0:T(8,128)(2,1)S(1)}, bf16[576,1728]{1,0:T(8,128)(2,1)}, u32[]{:S(2)}) copy-start(bf16[576,1728]{1,0:T(8,128)(2,1)} %reshape.267) | copy-start | bytes 5971972
  409.4 3.9 slice-start
  410.5 2.8 slice-start.1
  (35 other events, 55.7 us)
Sparse Core Ops, SparseCore 0:
  10.2 26.2 all-gather.3
  38.7 37.8 all-gather.5

commit v2 on v1

--- a/solution.py
+++ b/solution.py
@@ -2,6 +2,9 @@
 import jax.numpy as jnp
 from jax import lax
 from jax.sharding import PartitionSpec as P
+from jax.experimental import pallas as pl
+from jax.experimental.pallas import tpu as pltpu
+import functools
 
 GROUPS = 32
 EPS = 1e-06
@@ -61,21 +64,48 @@
     return jnp.transpose(weight, (2, 3, 0, 1, 4)).reshape(3 * outputs, 9 * channels)
 
 
-def causal_conv(window, taps, rows_out):
-    channels = window.shape[1]
-    columns = window.shape[3]
+def conv_body(x0, x1, x2, taps, bias, *rest, rows_out, pair, with_res):
+    if with_res:
+        res, out = rest
+    else:
+        (out,) = rest
+    outputs = out.shape[1]
+    columns = out.shape[2]
+    lanes = pair * columns
+    lane = lax.broadcasted_iota(jnp.int32, (outputs, lanes), 1) % columns
+
+    def step(i, carry):
+        r = i * pair
+        cols = []
+        for k in range(pair):
+            parts = [x0[pl.ds(r + k, 3)], x1[pl.ds(r + k, 3)], x2[pl.ds(r + k, 3)]]
+            cols.append(jnp.concatenate(parts, axis=0).reshape(9 * x0.shape[1], columns))
+        rhs = cols[0] if pair == 1 else jnp.concatenate(cols, axis=1)
+        acc = jnp.dot(taps[...], rhs, preferred_element_type=jnp.float32)
+        left = pltpu.roll(acc[:outputs], 1, 1)
+        right = pltpu.roll(acc[2 * outputs :], lanes - 1, 1)
+        total = acc[outputs : 2 * outputs] + jnp.where(lane == 0, 0.0, left)
+        total = total + jnp.where(lane == columns - 1, 0.0, right) + bias[...]
+        for k in range(pair):
+            piece = total[:, k * columns : (k + 1) * columns]
+            if with_res:
+                piece = piece + res[r + k].astype(jnp.float32)
+            out[r + k] = piece.astype(out.dtype)
+        return carry
+
+    lax.fori_loop(0, rows_out // pair, step, 0)
+
+
+def causal_conv(x0, x1, x2, taps, bias_vec, res=None):
+    rows_out = x0.shape[0] - 2
     outputs = taps.shape[0] // 3
-    pieces = [
-        window[step_t, :, step_y : step_y + rows_out, :]
-        for step_t in range(3)
-        for step_y in range(3)
-    ]
-    stacked = jnp.stack(pieces).reshape(9 * channels, rows_out * columns)
-    running = jnp.dot(taps, stacked, preferred_element_type=jnp.float32)
-    running = running.reshape(3, outputs, rows_out, columns)
-    leftward = jnp.pad(running[0, :, :, :-1], ((0, 0), (0, 0), (1, 0)))
-    rightward = jnp.pad(running[2, :, :, 1:], ((0, 0), (0, 0), (0, 1)))
-    return running[1] + leftward + rightward
+    pair = 4 if rows_out % 4 == 0 else (2 if rows_out % 2 == 0 else 1)
+    args = [x0, x1, x2, taps, bias_vec.reshape(outputs, 1)]
+    if res is not None:
+        args.append(res)
+    body = functools.partial(conv_body, rows_out=rows_out, pair=pair, with_res=res is not None)
+    shape = jax.ShapeDtypeStruct((rows_out, outputs, x0.shape[2]), jnp.bfloat16)
+    return pl.pallas_call(body, out_shape=shape)(*args)
 
 
 def block_sum(values, span_count):
@@ -87,26 +117,25 @@
 
 
 def activate(source, gain_vec, shift_vec, cell_count, span_count):
-    channels, height, columns = source.shape
-    grouped = source.astype(jnp.float32).reshape(GROUPS, channels // GROUPS, height, columns)
-    average = block_sum(jnp.sum(grouped, axis=(1, 2, 3)), span_count) / cell_count
-    centred = grouped - average[:, None, None, None]
-    spread = block_sum(jnp.sum(centred * centred, axis=(1, 2, 3)), span_count) / cell_count
+    height, channels, columns = source.shape
+    grouped = source.astype(jnp.float32).reshape(height, GROUPS, channels // GROUPS, columns)
+    average = block_sum(jnp.sum(grouped, axis=(0, 2, 3)), span_count) / cell_count
+    centred = grouped - average[None, :, None, None]
+    spread = block_sum(jnp.sum(centred * centred, axis=(0, 2, 3)), span_count) / cell_count
     inverse = lax.rsqrt(spread + EPS)
-    normed = (centred * inverse[:, None, None, None]).reshape(channels, height, columns)
-    normed = normed * gain_vec[:, None, None] + shift_vec[:, None, None]
+    normed = (centred * inverse[None, :, None, None]).reshape(height, channels, columns)
+    normed = normed * gain_vec[None, :, None] + shift_vec[None, :, None]
     return jax.nn.silu(normed).astype(jnp.bfloat16)
 
 
 def run_frame(source, first_hist, second_hist, kernels, biases, gains, shifts, cell_count, span_count):
-    span = source.shape[1]
-    first_in = with_rim(activate(source, gains[0], shifts[0], cell_count, span_count), 1, span_count)
-    first_win = jnp.concatenate([first_hist, first_in[None]], axis=0)
-    hidden = (causal_conv(first_win, kernels[0], span) + biases[0][:, None, None]).astype(jnp.bfloat16)
-    second_in = with_rim(activate(hidden, gains[1], shifts[1], cell_count, span_count), 1, span_count)
-    second_win = jnp.concatenate([second_hist, second_in[None]], axis=0)
-    result = causal_conv(second_win, kernels[1], span) + biases[1][:, None, None] + source.astype(jnp.float32)
-    return (result.astype(jnp.bfloat16), first_win[1:], second_win[1:])
+    first_in = with_rim(activate(source, gains[0], shifts[0], cell_count, span_count), 0, span_count)
+    hidden = causal_conv(first_hist[0], first_hist[1], first_in, kernels[0], biases[0])
+    second_in = with_rim(activate(hidden, gains[1], shifts[1], cell_count, span_count), 0, span_count)
+    result = causal_conv(second_hist[0], second_hist[1], second_in, kernels[1], biases[1], source)
+    first_next = jnp.stack([first_hist[1], first_in])
+    second_next = jnp.stack([second_hist[1], second_in])
+    return (result, first_next, second_next)
 
 
 def shards(frames, causal_cache, conv_weight, conv_bias, norm_gain, norm_shift):
@@ -120,9 +149,9 @@
     span_count = span_devices(peers, rows_here)
     span = rows_here * span_count
     cell_count = float(channels // GROUPS * rows_here * peers * columns)
-    frames_span = gather_span(frames, 2, span_count)
-    cache_span = gather_span(causal_cache[0], 3, span_count)
-    rimmed = with_rim(cache_span, 3, span_count)
+    frames_span = gather_span(jnp.transpose(frames, (0, 2, 1, 3)), 1, span_count)
+    cache_span = gather_span(jnp.transpose(causal_cache[0], (0, 1, 3, 2, 4)), 2, span_count)
+    rimmed = with_rim(cache_span, 2, span_count)
     first_hist = rimmed[0]
     second_hist = rimmed[1]
     local_taps = (arrange_taps(conv_weight[0, 0]), arrange_taps(conv_weight[0, 1]))
@@ -146,9 +175,11 @@
         if tick_no + 1 < tick_count:
             incoming = lax.ppermute(result, "phase", [(s, s + 1) for s in range(phase_count - 1)])
     start = (lax.axis_index("rows") % span_count) * rows_here
-    new_cache = jnp.stack([first_hist[:, :, 1 : 1 + span, :], second_hist[:, :, 1 : 1 + span, :]])
-    produced = lax.dynamic_slice_in_dim(produced, start, rows_here, axis=2)
-    new_cache = lax.dynamic_slice_in_dim(new_cache, start, rows_here, axis=3)
+    new_cache = jnp.stack([first_hist, second_hist])
+    produced = lax.dynamic_slice_in_dim(produced, start, rows_here, axis=1)
+    new_cache = lax.dynamic_slice_in_dim(new_cache, start + 1, rows_here, axis=2)
+    produced = jnp.transpose(produced, (0, 2, 1, 3))
+    new_cache = jnp.transpose(new_cache, (0, 1, 3, 2, 4))
     return (produced[None], new_cache[None])
 
 

time: 442 us -> 354 us (0.80)
  local copies, waits for them, and re-layouts: 197 us -> 87.9 us
  Pallas kernels: 0 us -> 88.4 us
  matrix products: 55.6 us -> 0 us
  waiting for transfers between devices: 97.8 us -> 71.5 us
  other arithmetic: 60.2 us -> 76 us
    pallas_call x0 -> x10, Pallas kernels: none -> 88.4 us  [causal_conv(): return pl.pallas_call(body, out_shape=shape)(*args)]
    unnamed x266 -> x80, local copies, waits for them, and re-layouts: 66.5 us -> 8.64 us
    dot_general x10 -> x0, matrix products: 55.6 us -> none  [causal_conv(): running = jnp.dot(taps, stacked, preferred_element_type=jnp.float32)]
    another operation x20 -> x21, local copies, waits for them, and re-layouts: 83 us -> 39.9 us  [the longest x9 19.6 us: run_frame(): first_next = jnp.stack([first_hist[1], first_in])]
    ppermute x4, waiting for transfers between devices: 59.6 us -> 40.5 us  [shards(): lax.ppermute(result, 'phase', [(s, s + 1) for s in range(phase_count - 1)])]
    all_gather x2, waiting for transfers between devices: 38.2 us -> 30.9 us  [gather_span(): return lax.all_gather(array, 'rows', axis=dim, tiled=True)]
    select_n x3 -> x4, other arithmetic: 0.69 us -> 7.4 us  [shards(): second_hist = jnp.where(active_now, second_next, second_hist)]
    select_n x5, other arithmetic: 4.98 us -> 11.5 us  [shards(): jnp.where(active_now, lax.dynamic_update_index_in_dim(produced, result, f...]
  transfers between devices with their start and end apart: 6 -> 6, of which waited for: 6 -> 5; matrix products, arithmetic and copies ran while one was open for 8% -> 20% of each run, Pallas kernels for 0% -> 0%
where the time goes in v2:
time: 354 us; the launch traced here: 349 us
  Pallas kernels  88.4 us (25%)
  local copies, waits for them, and re-layouts  87.9 us (25%)
  other arithmetic  76 us (21%)
  waiting for transfers between devices  71.5 us (20%)
  between operations  15.2 us (4%)
  starting transfers between devices  10.2 us (3%)
    pallas_call x10, Pallas kernels, causal_conv(): return pl.pallas_call(body, out_shape=shape)(*args)  88.4 us
    ppermute x4, waiting for transfers between devices, shards(): lax.ppermute(result, 'phase', [(s, s + 1) for s in range(phase_count - 1)])  40.5 us
    all_gather x2, waiting for transfers between devices, gather_span(): return lax.all_gather(array, 'rows', axis=dim, tiled=True)  30.9 us
    convert_element_type x10, other arithmetic, activate(): return jax.nn.silu(normed).astype(jnp.bfloat16)  19.7 us
    another operation x9, local copies, waits for them, and re-layouts, run_frame(): first_next = jnp.stack([first_hist[1], first_in])  19.6 us
    another operation x9, local copies, waits for them, and re-layouts, run_frame(): second_next = jnp.stack([second_hist[1], second_in])  18.8 us
    reduce_sum x20, other arithmetic, activate(): jnp.sum(centred * centred, axis=(0, 2, 3))  16 us
    reshape x2, local copies, waits for them, and re-layouts, arrange_taps(): jnp.transpose(weight, (2, 3, 0, 1, 4)).reshape(3 * outputs, 9 * channels)  14 us
  transfers between devices with their start and end apart: 6, of which 5 were waited for; matrix products, arithmetic and copies ran while one was open for 20% of the time, Pallas kernels for 0%

profile of v2, /device:TPU:4, one launch (start us, length us, event | category | flops | bytes accessed | tf_op | source)
XLA Modules:
  0.0 349.1 jit_solution(14391987452107343866)
XLA Ops:
  10.8 3.2 slice_bitcast_fusion
  13.9 4.0 %copy.16 = bf16[3,192,3,3,192]{4,3,2,1,0:T(4,128)(2,1)} copy(bf16[3,192,3,3,192]{4,1,0,3,2:T(8,128)(2,1)S(1)} %get-tuple-element.17) | data formatting | bytes 3981312 | tf_op jit(solution)/shard_map/transpose | solution.py:64
  18.0 7.1 %reshape.222.taps = bf16[576,1728]{1,0:T(8,128)(2,1)} reshape(bf16[3,192,3,3,192]{4,3,2,1,0:T(4,128)(2,1)} %copy.16) | data formatting | bytes 3981312 | tf_op jit(solution)/shard_map/reshape | solution.py:64
  25.8 4.1 %copy.18 = bf16[3,192,3,3,192]{4,3,2,1,0:T(4,128)(2,1)} copy(bf16[3,192,3,3,192]{4,1,0,3,2:T(8,128)(2,1)S(1)} %get-tuple-element.16) | data formatting | bytes 3981312 | tf_op jit(solution)/shard_map/transpose | solution.py:64
  29.9 6.9 %reshape.223.taps = bf16[576,1728]{1,0:T(8,128)(2,1)} reshape(bf16[3,192,3,3,192]{4,3,2,1,0:T(4,128)(2,1)} %copy.18) | data formatting | bytes 3981312 | tf_op jit(solution)/shard_map/reshape | solution.py:64
  43.5 2.2 pad_bitcast_fusion.16
  45.6 30.9 %all-gather.3.cloned.1.call-done = bf16[2,2,16,192,128]{4,3,2,1,0:T(8,128)(2,1)} async-done(((bf16[2,2,2,192,128]{4,3,2,1,0:T(8,128)(2,1)}), bf16[2,2,16,192,128]{4,3,2,1,0:T(8,128)(2,1)}) %all-gather.3.cloned.1.call-update) | async-done | bytes 3145744 | tf_op jit(solution)/shard_map/all_gather | solution.py:26
  76.5 5.9 %pad_slice_fusion.2 = (bf16[1,1,18,192,128]{4,3,2,1,0:T(8,128)(2,1)}, bf16[18,192,128]{2,1,0:T(8,128)(2,1)}, bf16[1,18,192,128]{3,2,1,0:T(8,128)(2,1)}, bf16[18,...) fusion(bf16[2,2,16,192,128]{4,3,2,1,0:T(8,128)(2,1)} %all-gathe, ...), kind=kLoop, calls=%fused_computation.6 | loop fusion | bytes 10223616 | tf_op jit(solution)/shard_map/slice | solution.py:133
  82.4 8.6 %shard_map.77 = bf16[16,192,128]{2,1,0:T(8,128)(2,1)} custom-call(bf16[18,192,128]{2,1,0:T(8,128)(2,1)} %get-tuple-element.24.x0, bf16[18,192,128]{2,1,0:T(8,128)(2,1)} %get-tuple-element.19.x1, bf16[18,192,128]{2,1,0:T(8,128)(2,1)} %get-tuple-element.60.x2, bf16[576,1728]{1,0:T(8,128)(2,1)} %reshape.222.taps, f32[192,1]{1,0:T(8,128)} %copy.17.bias), custom_call_target="tpu_custom_call" | custom-call | tf_op jit(solution)/shard_map/pallas_call | solution.py:108
  95.7 2.1 pad_bitcast_fusion.14
  97.8 9.1 %shard_map.78 = bf16[16,192,128]{2,1,0:T(8,128)(2,1)} custom-call(bf16[18,192,128]{2,1,0:T(8,128)(2,1)} %get-tuple-element.25.x0, bf16[18,192,128]{2,1,0:T(8,128)(2,1)} %get-tuple-element.21.x1, bf16[18,192,128]{2,1,0:T(8,128)(2,1)} %get-tuple-element.74.x2, bf16[576,1728]{1,0:T(8,128)(2,1)} %reshape.223.taps, f32[192,1]{1,0:T(8,128)} %copy.19.bias, ...), custom_call_target="tpu_custom_call" | custom-call | tf_op jit(solution)/shard_map/pallas_call | solution.py:108
  106.9 3.4 collective-permute-start
  110.3 2.5 maximum_select_fusion.1
  115.6 2.5 slice_bitcast_fusion.27
  118.1 2.6 slice_bitcast_fusion.25
  120.7 8.9 %collective-permute-done = bf16[16,192,128]{2,1,0:T(8,128)(2,1)S(1)} collective-permute-done((bf16[16,192,128]{2,1,0:T(8,128)(2,1)}, bf16[16,192,128]{2,1,0:T(8,128)(2,1)S(1)}, u32[]{:S(2)}, u32[]{:S(2)}) %collective-permute-start) | collective-permute-done | bytes 786464 | tf_op jit(solution)/shard_map/ppermute | solution.py:176
  133.1 2.1 fusion.89
  137.3 8.7 %shard_map.79 = bf16[16,192,128]{2,1,0:T(8,128)(2,1)} custom-call(bf16[18,192,128]{2,1,0:T(8,128)(2,1)} %get-tuple-element.31.x0, bf16[18,192,128]{2,1,0:T(8,128)(2,1)} %get-tuple-element.29.x1, bf16[18,192,128]{2,1,0:T(8,128)(2,1)} %get-tuple-element.63.x2, bf16[576,1728]{1,0:T(8,128)(2,1)} %reshape.222.taps, f32[192,1]{1,0:T(8,128)} %copy.17.bias), custom_call_target="tpu_custom_call" | custom-call | tf_op jit(solution)/shard_map/pallas_call | solution.py:108
  149.6 2.1 fusion.80
  151.7 2.2 pad_bitcast_fusion.10
  153.9 8.9 %shard_map.80 = bf16[16,192,128]{2,1,0:T(8,128)(2,1)} custom-call(bf16[18,192,128]{2,1,0:T(8,128)(2,1)} %get-tuple-element.46.x0, bf16[18,192,128]{2,1,0:T(8,128)(2,1)} %get-tuple-element.44.x1, bf16[18,192,128]{2,1,0:T(8,128)(2,1)} %get-tuple-element.77.x2, bf16[576,1728]{1,0:T(8,128)(2,1)} %reshape.223.taps, f32[192,1]{1,0:T(8,128)} %copy.19.bias, ...), custom_call_target="tpu_custom_call" | custom-call | tf_op jit(solution)/shard_map/pallas_call | solution.py:108
  162.8 2.5 collective-permute-start.1
  165.3 3.5 maximum_select_fusion.2
  168.8 2.8 fusion.106
  171.6 2.5 slice_bitcast_fusion.23
  174.1 2.4 slice_bitcast_fusion.21
  176.5 8.1 %collective-permute-done.1 = bf16[16,192,128]{2,1,0:T(8,128)(2,1)S(1)} collective-permute-done((bf16[16,192,128]{2,1,0:T(8,128)(2,1)}, bf16[16,192,128]{2,1,0:T(8,128)(2,1)S(1)}, u32[]{:S(2)}, u32[]{:S(2)}) %collective-permute-start.1) | collective-permute-done | bytes 786464 | tf_op jit(solution)/shard_map/ppermute | solution.py:176
  188.2 2.1 fusion.71
  190.3 2.1 pad_bitcast_fusion.8
  192.4 9.0 %shard_map.81 = bf16[16,192,128]{2,1,0:T(8,128)(2,1)} custom-call(bf16[18,192,128]{2,1,0:T(8,128)(2,1)} %get-tuple-element.35.x0, bf16[18,192,128]{2,1,0:T(8,128)(2,1)} %get-tuple-element.33.x1, bf16[18,192,128]{2,1,0:T(8,128)(2,1)} %get-tuple-element.66.x2, bf16[576,1728]{1,0:T(8,128)(2,1)} %reshape.222.taps, f32[192,1]{1,0:T(8,128)} %copy.17.bias), custom_call_target="tpu_custom_call" | custom-call | tf_op jit(solution)/shard_map/pallas_call | solution.py:108
  209.8 2.4 slice_bitcast_fusion.19
  212.2 8.9 %shard_map.82 = bf16[16,192,128]{2,1,0:T(8,128)(2,1)} custom-call(bf16[18,192,128]{2,1,0:T(8,128)(2,1)} %get-tuple-element.50.x0, bf16[18,192,128]{2,1,0:T(8,128)(2,1)} %get-tuple-element.48.x1, bf16[18,192,128]{2,1,0:T(8,128)(2,1)} %get-tuple-element.80.x2, bf16[576,1728]{1,0:T(8,128)(2,1)} %reshape.223.taps, f32[192,1]{1,0:T(8,128)} %copy.19.bias, ...), custom_call_target="tpu_custom_call" | custom-call | tf_op jit(solution)/shard_map/pallas_call | solution.py:108
  223.2 2.5 fusion.105
  227.3 2.5 slice_bitcast_fusion.17
  229.8 12.4 %collective-permute-done.2 = bf16[16,192,128]{2,1,0:T(8,128)(2,1)S(1)} collective-permute-done((bf16[16,192,128]{2,1,0:T(8,128)(2,1)}, bf16[16,192,128]{2,1,0:T(8,128)(2,1)S(1)}, u32[]{:S(2)}, u32[]{:S(2)}) %collective-permute-start.2) | collective-permute-done | bytes 786464 | tf_op jit(solution)/shard_map/ppermute | solution.py:176
  247.8 2.1 pad_bitcast_fusion.4
  250.0 8.6 %shard_map.83 = bf16[16,192,128]{2,1,0:T(8,128)(2,1)} custom-call(bf16[18,192,128]{2,1,0:T(8,128)(2,1)} %get-tuple-element.39.x0, bf16[18,192,128]{2,1,0:T(8,128)(2,1)} %get-tuple-element.37.x1, bf16[18,192,128]{2,1,0:T(8,128)(2,1)} %get-tuple-element.69.x2, bf16[576,1728]{1,0:T(8,128)(2,1)} %reshape.222.taps, f32[192,1]{1,0:T(8,128)} %copy.17.bias), custom_call_target="tpu_custom_call" | custom-call | tf_op jit(solution)/shard_map/pallas_call | solution.py:108
  262.3 2.2 fusion.44
  269.0 8.9 %shard_map.84 = bf16[16,192,128]{2,1,0:T(8,128)(2,1)} custom-call(bf16[18,192,128]{2,1,0:T(8,128)(2,1)} %get-tuple-element.54.x0, bf16[18,192,128]{2,1,0:T(8,128)(2,1)} %get-tuple-element.52.x1, bf16[18,192,128]{2,1,0:T(8,128)(2,1)} %get-tuple-element.83.x2, bf16[576,1728]{1,0:T(8,128)(2,1)} %reshape.223.taps, f32[192,1]{1,0:T(8,128)} %copy.19.bias, ...), custom_call_target="tpu_custom_call" | custom-call | tf_op jit(solution)/shard_map/pallas_call | solution.py:108
  277.9 2.2 collective-permute-start.3
  280.1 2.5 fusion.104
  282.6 2.3 maximum_select_fusion.7
  286.9 11.2 %collective-permute-done.3 = bf16[16,192,128]{2,1,0:T(8,128)(2,1)S(1)} collective-permute-done((bf16[16,192,128]{2,1,0:T(8,128)(2,1)}, bf16[16,192,128]{2,1,0:T(8,128)(2,1)S(1)}, u32[]{:S(2)}, u32[]{:S(2)}) %collective-permute-start.3) | collective-permute-done | bytes 786464 | tf_op jit(solution)/shard_map/ppermute | solution.py:176
  301.6 2.1 fusion.35
  305.3 8.7 %shard_map.85 = bf16[16,192,128]{2,1,0:T(8,128)(2,1)} custom-call(bf16[18,192,128]{2,1,0:T(8,128)(2,1)} %get-tuple-element.42.x0, bf16[18,192,128]{2,1,0:T(8,128)(2,1)} %get-tuple-element.41.x1, bf16[18,192,128]{2,1,0:T(8,128)(2,1)} %get-tuple-element.71.x2, bf16[576,1728]{1,0:T(8,128)(2,1)} %reshape.222.taps, f32[192,1]{1,0:T(8,128)} %copy.17.bias), custom_call_target="tpu_custom_call" | custom-call | tf_op jit(solution)/shard_map/pallas_call | solution.py:108
  321.3 9.0 %shard_map.86 = bf16[16,192,128]{2,1,0:T(8,128)(2,1)} custom-call(bf16[18,192,128]{2,1,0:T(8,128)(2,1)} %get-tuple-element.57.x0, bf16[18,192,128]{2,1,0:T(8,128)(2,1)} %get-tuple-element.56.x1, bf16[18,192,128]{2,1,0:T(8,128)(2,1)} %get-tuple-element.85.x2, bf16[576,1728]{1,0:T(8,128)(2,1)} %reshape.223.taps, f32[192,1]{1,0:T(8,128)} %copy.19.bias, ...), custom_call_target="tpu_custom_call" | custom-call | tf_op jit(solution)/shard_map/pallas_call | solution.py:108
  330.3 2.6 fusion.103
  334.8 3.4 maximum_select_fusion.13
  (231 shorter events, 76.8 us)
Async XLA Ops:
  7.2 30.5 %all-gather.5.cloned.1.call-start = ((), (), s32[]{:S(2)}) async-start(), calls=%async_computation.1 | async-start | bytes 1769472 | tf_op jit(solution)/shard_map/all_gather | solution.py:26
  8.9 67.6 %all-gather.3.cloned.1.call-start = ((), (), s32[]{:S(2)}) async-start(), calls=%async_computation | async-start | bytes 3538944 | tf_op jit(solution)/shard_map/all_gather | solution.py:26
  18.0 7.1 %copy-start.35 = (f32[1,2,192]{2,1,0:T(2,128)S(1)}, f32[1,2,192]{2,1,0:T(2,128)}, u32[]{:S(2)}) copy-start(f32[1,2,192]{2,1,0:T(2,128)} %param.9) | copy-start | bytes 4612
  29.9 7.7 %copy-start.36 = (f32[1,2,192]{2,1,0:T(2,128)S(1)}, f32[1,2,192]{2,1,0:T(2,128)}, u32[]{:S(2)}) copy-start(f32[1,2,192]{2,1,0:T(2,128)} %param.11) | copy-start | bytes 4612
  29.9 7.7 %copy-start.37 = (f32[1,2,192]{2,1,0:T(2,128)S(1)}, f32[1,2,192]{2,1,0:T(2,128)}, u32[]{:S(2)}) copy-start(f32[1,2,192]{2,1,0:T(2,128)} %param.10) | copy-start | bytes 4612
  37.7 3.9 %copy-start.7 = (bf16[2,16,192,128]{3,2,1,0:T(8,128)(2,1)S(1)}, bf16[2,16,192,128]{3,2,1,0:T(8,128)(2,1)}, u32[]{:S(2)}) copy-start(bf16[2,16,192,128]{3,2,1,0:T(8,128)(2,1)} %all-gather.5.cloned.1.call-done) | copy-start | bytes 4718596
  91.0 3.7 %copy-start.14 = (bf16[16,192,128]{2,1,0:T(8,128)(2,1)S(1)}, bf16[16,192,128]{2,1,0:T(8,128)(2,1)}, u32[]{:S(2)}) copy-start(bf16[16,192,128]{2,1,0:T(8,128)(2,1)} %shard_map.77) | copy-start | bytes 2359300
  97.8 12.4 %copy-start = (bf16[2,2,16,192,128]{4,3,2,1,0:T(8,128)(2,1)S(1)}, bf16[2,2,16,192,128]{4,3,2,1,0:T(8,128)(2,1)}, u32[]{:S(2)}) copy-start(bf16[2,2,16,192,128]{4,3,2,1,0:T(8,128)(2,1)} %all-gather.3.cloned.1.call-done) | copy-start | bytes 9437188
  106.9 22.7 %collective-permute-start = (bf16[16,192,128]{2,1,0:T(8,128)(2,1)}, bf16[16,192,128]{2,1,0:T(8,128)(2,1)S(1)}, u32[]{:S(2)}, u32[]{:S(2)}) collective-permute-start(bf16[16,192,128]{2,1,0:T(8,128)(2,1)} %shard_map.78), channel_id=1, source_target_pairs={{0,8},{8,16},{16,24},{1,9},{9,17},{17,25},{2,10},{10,18},{18,26},{... | collective-permute-start | bytes 2359304 | tf_op jit(solution)/shard_map/ppermute | solution.py:176
  112.8 5.3 %copy-start.13 = (bf16[2,18,192,128]{3,2,1,0:T(8,128)(2,1)}, bf16[2,18,192,128]{3,2,1,0:T(8,128)(2,1)S(1)}, u32[]{:S(2)}) copy-start(bf16[2,18,192,128]{3,2,1,0:T(8,128)(2,1)S(1)} %get-tuple-element.27) | copy-start | bytes 5308420
  112.8 5.3 %copy-start.12 = (bf16[2,18,192,128]{3,2,1,0:T(8,128)(2,1)}, bf16[2,18,192,128]{3,2,1,0:T(8,128)(2,1)S(1)}, u32[]{:S(2)}) copy-start(bf16[2,18,192,128]{3,2,1,0:T(8,128)(2,1)S(1)} %get-tuple-element.26) | copy-start | bytes 5308420
  112.8 1.7 copy-start.33
  118.1 11.5 %copy-start.8 = (bf16[2,16,192,128]{3,2,1,0:T(8,128)(2,1)S(1)}, bf16[2,16,192,128]{3,2,1,0:T(8,128)(2,1)}, u32[]{:S(2)}) copy-start(bf16[2,16,192,128]{3,2,1,0:T(8,128)(2,1)} %all-gather.5.cloned.1.call-done) | copy-start | bytes 4718596
  162.8 21.9 %collective-permute-start.1 = (bf16[16,192,128]{2,1,0:T(8,128)(2,1)}, bf16[16,192,128]{2,1,0:T(8,128)(2,1)S(1)}, u32[]{:S(2)}, u32[]{:S(2)}) collective-permute-start(bf16[16,192,128]{2,1,0:T(8,128)(2,1)} %shard_map.80), channel_id=1, source_target_pairs={{0,8},{8,16},{16,24},{1,9},{9,17},{17,25},{2,10},{10,18},{18,26},{... | collective-permute-start | bytes 2359304 | tf_op jit(solution)/shard_map/ppermute | solution.py:176
  165.3 3.5 %copy-start.34 = (bf16[16,192,128]{2,1,0:T(8,128)(2,1)S(1)}, bf16[16,192,128]{2,1,0:T(8,128)(2,1)}, u32[]{:S(2)}) copy-start(bf16[16,192,128]{2,1,0:T(8,128)(2,1)} %shard_map.80) | copy-start | bytes 2359300
  168.8 5.3 %copy-start.4 = (bf16[2,18,192,128]{3,2,1,0:T(8,128)(2,1)}, bf16[2,18,192,128]{3,2,1,0:T(8,128)(2,1)S(1)}, u32[]{:S(2)}) copy-start(bf16[2,18,192,128]{3,2,1,0:T(8,128)(2,1)S(1)} %get-tuple-element.92) | copy-start | bytes 5308420
  168.8 5.3 %copy-start.1 = (bf16[2,18,192,128]{3,2,1,0:T(8,128)(2,1)}, bf16[2,18,192,128]{3,2,1,0:T(8,128)(2,1)S(1)}, u32[]{:S(2)}) copy-start(bf16[2,18,192,128]{3,2,1,0:T(8,128)(2,1)S(1)} %get-tuple-element.93) | copy-start | bytes 5308420
  174.1 10.6 %copy-start.9 = (bf16[2,16,192,128]{3,2,1,0:T(8,128)(2,1)S(1)}, bf16[2,16,192,128]{3,2,1,0:T(8,128)(2,1)}, u32[]{:S(2)}) copy-start(bf16[2,16,192,128]{3,2,1,0:T(8,128)(2,1)} %all-gather.5.cloned.1.call-done) | copy-start | bytes 4718596
  207.1 1.7 copy-start.5
  207.1 2.3 copy-start.17
  208.9 0.9 copy-start.15
  221.1 4.5 %copy-start.2 = (bf16[2,18,192,128]{3,2,1,0:T(8,128)(2,1)S(1)}, bf16[2,18,192,128]{3,2,1,0:T(8,128)(2,1)}, u32[]{:S(2)}) copy-start(bf16[2,18,192,128]{3,2,1,0:T(8,128)(2,1)} %copy-done.1) | copy-start | bytes 5308420
  221.1 21.1 %collective-permute-start.2 = (bf16[16,192,128]{2,1,0:T(8,128)(2,1)}, bf16[16,192,128]{2,1,0:T(8,128)(2,1)S(1)}, u32[]{:S(2)}, u32[]{:S(2)}) collective-permute-start(bf16[16,192,128]{2,1,0:T(8,128)(2,1)} %shard_map.82), channel_id=1, source_target_pairs={{0,8},{8,16},{16,24},{1,9},{9,17},{17,25},{2,10},{10,18},{18,26},{... | collective-permute-start | bytes 2359304 | tf_op jit(solution)/shard_map/ppermute | solution.py:176
  227.3 14.9 %copy-start.10 = (bf16[2,16,192,128]{3,2,1,0:T(8,128)(2,1)S(1)}, bf16[2,16,192,128]{3,2,1,0:T(8,128)(2,1)}, u32[]{:S(2)}) copy-start(bf16[2,16,192,128]{3,2,1,0:T(8,128)(2,1)} %all-gather.5.cloned.1.call-done) | copy-start | bytes 4718596
  262.3 4.1 %copy-start.18 = (bf16[1,18,192,128]{3,2,1,0:T(8,128)(2,1)S(1)}, bf16[1,18,192,128]{3,2,1,0:T(8,128)(2,1)}, u32[]{:S(2)}) copy-start(bf16[1,18,192,128]{3,2,1,0:T(8,128)(2,1)} %get-tuple-element.49) | copy-start | bytes 2654212
  262.3 4.1 %copy-start.32 = (bf16[1,18,192,128]{3,2,1,0:T(8,128)(2,1)S(1)}, bf16[1,18,192,128]{3,2,1,0:T(8,128)(2,1)}, u32[]{:S(2)}) copy-start(bf16[1,18,192,128]{3,2,1,0:T(8,128)(2,1)} %get-tuple-element.53) | copy-start | bytes 2654212
  264.5 1.9 copy-start.6
  264.5 2.1 copy-start.16
  277.9 4.7 %copy-start.3 = (bf16[2,18,192,128]{3,2,1,0:T(8,128)(2,1)S(1)}, bf16[2,18,192,128]{3,2,1,0:T(8,128)(2,1)}, u32[]{:S(2)}) copy-start(bf16[2,18,192,128]{3,2,1,0:T(8,128)(2,1)} %copy-done.1) | copy-start | bytes 5308420
  277.9 20.1 %collective-permute-start.3 = (bf16[16,192,128]{2,1,0:T(8,128)(2,1)}, bf16[16,192,128]{2,1,0:T(8,128)(2,1)S(1)}, u32[]{:S(2)}, u32[]{:S(2)}) collective-permute-start(bf16[16,192,128]{2,1,0:T(8,128)(2,1)} %shard_map.84), channel_id=1, source_target_pairs={{0,8},{8,16},{16,24},{1,9},{9,17},{17,25},{2,10},{10,18},{18,26},{... | collective-permute-start | bytes 2359304 | tf_op jit(solution)/shard_map/ppermute | solution.py:176
  284.9 13.2 %copy-start.11 = (bf16[2,16,192,128]{3,2,1,0:T(8,128)(2,1)S(1)}, bf16[2,16,192,128]{3,2,1,0:T(8,128)(2,1)}, u32[]{:S(2)}) copy-start(bf16[2,16,192,128]{3,2,1,0:T(8,128)(2,1)} %all-gather.5.cloned.1.call-done) | copy-start | bytes 4718596
  330.3 4.5 %copy-start.20 = (bf16[1,1,18,192,128]{4,3,2,1,0:T(8,128)(2,1)S(1)}, bf16[1,1,18,192,128]{4,3,2,1,0:T(8,128)(2,1)}, u32[]{:S(2)}) copy-start(bf16[1,1,18,192,128]{4,3,2,1,0:T(8,128)(2,1)} %get-tuple-element.23) | copy-start | bytes 2654212
  330.3 4.5 %copy-start.22 = (bf16[1,1,18,192,128]{4,3,2,1,0:T(8,128)(2,1)S(1)}, bf16[1,1,18,192,128]{4,3,2,1,0:T(8,128)(2,1)}, u32[]{:S(2)}) copy-start(bf16[1,1,18,192,128]{4,3,2,1,0:T(8,128)(2,1)} %get-tuple-element.84) | copy-start | bytes 2654212
  330.3 4.5 %copy-start.24 = (bf16[1,1,18,192,128]{4,3,2,1,0:T(8,128)(2,1)S(1)}, bf16[1,1,18,192,128]{4,3,2,1,0:T(8,128)(2,1)}, u32[]{:S(2)}) copy-start(bf16[1,1,18,192,128]{4,3,2,1,0:T(8,128)(2,1)} %get-tuple-element.72) | copy-start | bytes 2654212
  334.8 3.5 copy-start.19
  334.8 3.5 copy-start.21
  334.8 3.6 %copy-start.23 = (bf16[1,1,18,192,128]{4,3,2,1,0:T(8,128)(2,1)S(1)}, bf16[1,1,18,192,128]{4,3,2,1,0:T(8,128)(2,1)}, u32[]{:S(2)}) copy-start(bf16[1,1,18,192,128]{4,3,2,1,0:T(8,128)(2,1)} %get-tuple-element.58) | copy-start | bytes 2654212
  334.8 3.8 %copy-start.25 = (bf16[1,1,18,192,128]{4,3,2,1,0:T(8,128)(2,1)S(1)}, bf16[1,1,18,192,128]{4,3,2,1,0:T(8,128)(2,1)}, u32[]{:S(2)}) copy-start(bf16[1,1,18,192,128]{4,3,2,1,0:T(8,128)(2,1)} %get-tuple-element.61) | copy-start | bytes 2654212
  334.8 4.1 %copy-start.26 = (bf16[1,1,18,192,128]{4,3,2,1,0:T(8,128)(2,1)S(1)}, bf16[1,1,18,192,128]{4,3,2,1,0:T(8,128)(2,1)}, u32[]{:S(2)}) copy-start(bf16[1,1,18,192,128]{4,3,2,1,0:T(8,128)(2,1)} %get-tuple-element.64) | copy-start | bytes 2654212
  334.8 4.3 %copy-start.27 = (bf16[1,1,18,192,128]{4,3,2,1,0:T(8,128)(2,1)S(1)}, bf16[1,1,18,192,128]{4,3,2,1,0:T(8,128)(2,1)}, u32[]{:S(2)}) copy-start(bf16[1,1,18,192,128]{4,3,2,1,0:T(8,128)(2,1)} %get-tuple-element.67) | copy-start | bytes 2654212
  334.8 4.6 %copy-start.28 = (bf16[1,1,18,192,128]{4,3,2,1,0:T(8,128)(2,1)S(1)}, bf16[1,1,18,192,128]{4,3,2,1,0:T(8,128)(2,1)}, u32[]{:S(2)}) copy-start(bf16[1,1,18,192,128]{4,3,2,1,0:T(8,128)(2,1)} %get-tuple-element.28) | copy-start | bytes 2654212
  334.8 4.8 %copy-start.29 = (bf16[1,1,18,192,128]{4,3,2,1,0:T(8,128)(2,1)S(1)}, bf16[1,1,18,192,128]{4,3,2,1,0:T(8,128)(2,1)}, u32[]{:S(2)}) copy-start(bf16[1,1,18,192,128]{4,3,2,1,0:T(8,128)(2,1)} %get-tuple-element.32) | copy-start | bytes 2654212
  334.8 5.1 %copy-start.30 = (bf16[1,1,18,192,128]{4,3,2,1,0:T(8,128)(2,1)S(1)}, bf16[1,1,18,192,128]{4,3,2,1,0:T(8,128)(2,1)}, u32[]{:S(2)}) copy-start(bf16[1,1,18,192,128]{4,3,2,1,0:T(8,128)(2,1)} %get-tuple-element.36) | copy-start | bytes 2654212
  334.8 5.3 %copy-start.31 = (bf16[1,1,18,192,128]{4,3,2,1,0:T(8,128)(2,1)S(1)}, bf16[1,1,18,192,128]{4,3,2,1,0:T(8,128)(2,1)}, u32[]{:S(2)}) copy-start(bf16[1,1,18,192,128]{4,3,2,1,0:T(8,128)(2,1)} %get-tuple-element.40) | copy-start | bytes 2654212
Sparse Core Ops, SparseCore 0:
  10.2 26.2 all-gather.4
  38.7 37.7 all-gather.2
